TPU v7x, 256 devices: a whole 4x4x8 slice. The times are simulated.
256 devices in a mesh: cx: 16 (over x, y), cy: 16 (over z, core).
Axes of the slice: x: 4, y: 4, z: 8, core: 2. Of those that a mesh axis runs over, the one named last changes fastest.
Arguments:
- query_rows: bfloat16 [65536, 1024], P(('cx', 'cy')), may hold values from -6 to 6
- key_rows: bfloat16 [65536, 1024], P(('cx', 'cy')), may hold values from -6 to 6
- value_rows: bfloat16 [65536, 1024], P(('cx', 'cy')), may hold values from -6 to 6
- forward_out: bfloat16 [65536, 1024], P(('cx', 'cy')), may hold values from -6 to 6
- out_grad: bfloat16 [65536, 1024], P(('cx', 'cy')), may hold values from -6 to 6
- doc_blocks: int32 [64], replicated, may hold values from 1 to 15, 512 in all
Outputs:
- query_grad: bfloat16 [65536, 1024], P(('cx', 'cy'))
- key_grad: bfloat16 [65536, 1024], P(('cx', 'cy'))
- value_grad: bfloat16 [65536, 1024], P(('cx', 'cy'))
Inputs may be any that keep to these rules, and one draw needn't show every extreme that they name: `doc_blocks`: lengths of the documents in blocks of 128 tokens, in sequence order, summing to 512; the longest has exactly 15 blocks.
All inputs are finite; a program needn't handle non-finite values.
Results may differ from a plain program's by a relative error of at most 0.0049.
Values may be sent and summed in bfloat16 or wider, within the bound.
No kernel may reach another device: no remote copies, remote signals or barrier semaphores. Data moves between devices by JAX's collectives and lax.ppermute only.
A program may use at most 128 MiB of HBM per device.

v0:
```python
import math

import jax
import jax.numpy as jnp
from jax import lax
from jax.sharding import PartitionSpec as P

HEADS = 8
DH = 128
BLOCK = 128
REACH = 7


def from_behind(value, axis, steps):
    count = lax.axis_size(axis)
    first, last = (max(0, -steps), min(count, count - steps))
    return lax.ppermute(value, axis, [(source, source + steps) for source in range(first, last)])


def doc_window(doc_blocks, first_block, count):
    ends = jnp.cumsum(doc_blocks)
    starts = ends - doc_blocks
    block_ids = first_block + jnp.arange(count, dtype=jnp.int32)
    found = jnp.sum((starts[None, :] <= block_ids[:, None]).astype(jnp.int32), axis=1) - 1
    return jnp.where(block_ids >= ends[-1], -2, found)


def per_device(query_rows, key_rows, value_rows, forward_out, out_grad, doc_blocks):
    rows, features = query_rows.shape
    scale = 1.0 / math.sqrt(DH)
    axes = ("cx", "cy")
    shard = lax.axis_index(axes)
    per_shard = rows // BLOCK
    window = REACH + 1
    block_docs = doc_window(doc_blocks, (shard - REACH) * per_shard, (2 * REACH + 1) * per_shard)
    token_docs = jnp.repeat(block_docs, BLOCK)

    def docs_at(step):
        return token_docs[(REACH + step) * rows : (REACH + step + 1) * rows]

    local_docs = docs_at(0)
    offsets = jnp.arange(rows, dtype=jnp.int32)
    causal = offsets[None, :] <= offsets[:, None]
    query_masks = [local_docs[:, None] == docs_at(-step)[None, :] for step in range(window)]
    query_masks[0] = query_masks[0] & causal
    key_masks = [local_docs[:, None] == docs_at(step)[None, :] for step in range(window)]

    def to_heads(x):
        return x.reshape(rows, HEADS, DH).transpose(1, 0, 2)

    def from_heads(x):
        return x.transpose(1, 0, 2).reshape(rows, features)

    query_h = to_heads(query_rows)
    grad_h = to_heads(out_grad)
    key_h = to_heads(key_rows)
    value_h = to_heads(value_rows)
    delta = jnp.einsum(
        "hqd,hqd->hq", grad_h, to_heads(forward_out), preferred_element_type=jnp.float32
    )

    key_values = [(key_h, value_h)]
    query_grads = [(query_h, grad_h)]
    moving_kv = (key_h, value_h)
    moving_qg = (query_h, grad_h)
    for step in range(1, window):
        moving_kv = from_behind(moving_kv, axes, 1)
        moving_qg = from_behind(moving_qg, axes, -1)
        key_values.append(moving_kv)
        query_grads.append(moving_qg)

    def scores_of(q, k, mask):
        s = jnp.einsum("hqd,hkd->hqk", q, k, preferred_element_type=jnp.float32) * scale
        return jnp.where(mask[None], s, -1e30)

    def tile_stats(q, k, mask):
        s = scores_of(q, k, mask)
        top = jnp.max(s, axis=2)
        return (top, jnp.sum(jnp.exp(s - top[..., None]), axis=2))

    def merged(step, stats):
        part = tile_stats(query_h, key_values[step][0], query_masks[step])
        top = jnp.maximum(stats[0], part[0])
        total = stats[1] * jnp.exp(stats[0] - top) + part[1] * jnp.exp(part[0] - top)
        return (top, total)

    stats = tile_stats(query_h, key_h, query_masks[0])
    for step in range(1, window):
        stats = merged(step, stats)
    logsum = stats[0] + jnp.log(stats[1])

    row_stats = jnp.concatenate([logsum, delta], axis=1)
    later_stats = [row_stats] + [from_behind(row_stats, axes, -step) for step in range(1, window)]

    def tile_grads(q, g, k, v, lse, dlt, mask):
        s = scores_of(q, k, mask)
        prob = jnp.where(mask[None], jnp.exp(s - lse[..., None]), 0.0)
        dprob = jnp.einsum("hqd,hkd->hqk", g, v, preferred_element_type=jnp.float32)
        dscore = (prob * (dprob - dlt[..., None])).astype(jnp.bfloat16)
        return prob.astype(jnp.bfloat16), dscore

    prob_b, dscore = lax.optimization_barrier(
        tile_grads(query_h, grad_h, key_h, value_h, logsum, delta, query_masks[0])
    )
    query_acc = jnp.einsum("hqk,hkd->hqd", dscore, key_h, preferred_element_type=jnp.float32)
    key_acc = jnp.einsum("hqk,hqd->hkd", dscore, query_h, preferred_element_type=jnp.float32)
    value_acc = jnp.einsum("hqk,hqd->hkd", prob_b, grad_h, preferred_element_type=jnp.float32)

    def query_tile(step, acc):
        k_in, v_in = key_values[step]
        dscore = lax.optimization_barrier(
            tile_grads(query_h, grad_h, k_in, v_in, logsum, delta, query_masks[step])[1]
        )
        return acc + jnp.einsum("hqk,hkd->hqd", dscore, k_in, preferred_element_type=jnp.float32)

    def key_tile(step, accs):
        q_in, g_in = query_grads[step]
        lse_in = later_stats[step][:, :rows]
        delta_in = later_stats[step][:, rows:]
        mask = key_masks[step]
        s = jnp.einsum("hkd,hqd->hkq", key_h, q_in, preferred_element_type=jnp.float32) * scale
        s = jnp.where(mask[None], s, -1e30)
        prob = jnp.where(mask[None], jnp.exp(s - lse_in[:, None, :]), 0.0)
        dprob = jnp.einsum("hkd,hqd->hkq", value_h, g_in, preferred_element_type=jnp.float32)
        dscore = (prob * (dprob - delta_in[:, None, :])).astype(jnp.bfloat16)
        prob_b, dscore = lax.optimization_barrier((prob.astype(jnp.bfloat16), dscore))
        k_part = jnp.einsum("hkq,hqd->hkd", dscore, q_in, preferred_element_type=jnp.float32)
        v_part = jnp.einsum("hkq,hqd->hkd", prob_b, g_in, preferred_element_type=jnp.float32)
        return (accs[0] + k_part, accs[1] + v_part)

    for step in range(1, window):
        query_acc = query_tile(step, query_acc)
        key_acc, value_acc = key_tile(step, (key_acc, value_acc))
    query_grad = from_heads(query_acc * scale).astype(jnp.bfloat16)
    key_grad = from_heads(key_acc * scale).astype(jnp.bfloat16)
    value_grad = from_heads(value_acc).astype(jnp.bfloat16)
    return (query_grad, key_grad, value_grad)


def solution(mesh):
    in_specs = (
        P(("cx", "cy"), None),
        P(("cx", "cy"), None),
        P(("cx", "cy"), None),
        P(("cx", "cy"), None),
        P(("cx", "cy"), None),
        P(),
    )
    out_specs = (P(("cx", "cy"), None), P(("cx", "cy"), None), P(("cx", "cy"), None))
    return jax.shard_map(
        per_device, mesh=mesh, in_specs=in_specs, out_specs=out_specs, check_vma=False
    )
```

profile of v0, /device:TPU:14, one launch (start us, length us, event | category | flops | bytes accessed | tf_op | source)
XLA Modules:
  0.0 223.1 jit_solution(11997470438998641103)
XLA Ops:
  4.7 4.1 %collective-permute-start.7 = (bf16[8,256,128]{2,1,0:T(8,128)(2,1)S(1)}, bf16[8,256,128]{2,1,0:T(8,128)(2,1)}, u32[]{:S(2)}, u32[]{:S(2)}) collective-permute-start(bf16[8,256,128]{2,1,0:T(8,128)(2,1)S(1)} %bitcast.234), channel_id=1, source_target_pairs={{0,1},{1,2},{2,3},{3,4},{4,5},{5,6},{6,7},{7,8},{8,9},{9,10},{10,1... | collective-permute-start | bytes 1572872 | tf_op jit(solution)/shard_map/ppermute | solution.py:17
  9.8 5.1 %collective-permute-start.14 = (bf16[8,256,128]{2,1,0:T(8,128)(2,1)S(1)}, bf16[8,256,128]{2,1,0:T(8,128)(2,1)}, u32[]{:S(2)}, u32[]{:S(2)}) collective-permute-start(bf16[8,256,128]{2,1,0:T(8,128)(2,1)S(1)} %bitcast.233), channel_id=1, source_target_pairs={{1,0},{2,1},{3,2},{4,3},{5,4},{6,5},{7,6},{8,7},{9,8},{10,9},{11,1... | collective-permute-start | bytes 1572872 | tf_op jit(solution)/shard_map/ppermute | solution.py:17
  16.5 2.6 %collective-permute-start.16 = (bf16[8,256,128]{2,1,0:T(8,128)(2,1)S(1)}, bf16[8,256,128]{2,1,0:T(8,128)(2,1)}, u32[]{:S(2)}, u32[]{:S(2)}) collective-permute-start(bf16[8,256,128]{2,1,0:T(8,128)(2,1)S(1)} %bitcast.232), channel_id=1, source_target_pairs={{1,0},{2,1},{3,2},{4,3},{5,4},{6,5},{7,6},{8,7},{9,8},{10,9},{11,1... | collective-permute-start | bytes 1572872 | tf_op jit(solution)/shard_map/ppermute | solution.py:17
  27.9 5.8 %collective-permute-start.17 = (bf16[8,256,128]{2,1,0:T(8,128)(2,1)}, bf16[8,256,128]{2,1,0:T(8,128)(2,1)}, u32[]{:S(2)}, u32[]{:S(2)}) collective-permute-start(bf16[8,256,128]{2,1,0:T(8,128)(2,1)} %collective-permute-done.14), channel_id=1, source_target_pairs={{1,0},{2,1},{3,2},{4,3},{5,4},{6,5},{7,6},{8,7},{9,8},{10,9},{11,1... | collective-permute-start | bytes 1572872 | tf_op jit(solution)/shard_map/ppermute | solution.py:17
  33.7 2.4 %collective-permute-start.19 = (bf16[8,256,128]{2,1,0:T(8,128)(2,1)}, bf16[8,256,128]{2,1,0:T(8,128)(2,1)}, u32[]{:S(2)}, u32[]{:S(2)}) collective-permute-start(bf16[8,256,128]{2,1,0:T(8,128)(2,1)} %collective-permute-done.16), channel_id=1, source_target_pairs={{1,0},{2,1},{3,2},{4,3},{5,4},{6,5},{7,6},{8,7},{9,8},{10,9},{11,1... | collective-permute-start | bytes 1572872 | tf_op jit(solution)/shard_map/ppermute | solution.py:17
  38.6 2.5 %collective-permute-done.8 = bf16[8,256,128]{2,1,0:T(8,128)(2,1)} collective-permute-done((bf16[8,256,128]{2,1,0:T(8,128)(2,1)}, bf16[8,256,128]{2,1,0:T(8,128)(2,1)}, u32[]{:S(2)}, u32[]{:S(2)}) %collective-permute-start.8) | collective-permute-done | bytes 524320 | tf_op jit(solution)/shard_map/ppermute | solution.py:17
  43.0 5.8 %collective-permute-start.20 = (bf16[8,256,128]{2,1,0:T(8,128)(2,1)}, bf16[8,256,128]{2,1,0:T(8,128)(2,1)}, u32[]{:S(2)}, u32[]{:S(2)}) collective-permute-start(bf16[8,256,128]{2,1,0:T(8,128)(2,1)} %collective-permute-done.17), channel_id=1, source_target_pairs={{1,0},{2,1},{3,2},{4,3},{5,4},{6,5},{7,6},{8,7},{9,8},{10,9},{11,1... | collective-permute-start | bytes 1572872 | tf_op jit(solution)/shard_map/ppermute | solution.py:17
  48.8 3.4 %collective-permute-start.22 = (bf16[8,256,128]{2,1,0:T(8,128)(2,1)}, bf16[8,256,128]{2,1,0:T(8,128)(2,1)}, u32[]{:S(2)}, u32[]{:S(2)}) collective-permute-start(bf16[8,256,128]{2,1,0:T(8,128)(2,1)} %collective-permute-done.19), channel_id=1, source_target_pairs={{1,0},{2,1},{3,2},{4,3},{5,4},{6,5},{7,6},{8,7},{9,8},{10,9},{11,1... | collective-permute-start | bytes 1572872 | tf_op jit(solution)/shard_map/ppermute | solution.py:17
  60.3 5.8 %collective-permute-start.23 = (bf16[8,256,128]{2,1,0:T(8,128)(2,1)}, bf16[8,256,128]{2,1,0:T(8,128)(2,1)S(1)}, u32[]{:S(2)}, u32[]{:S(2)}) collective-permute-start(bf16[8,256,128]{2,1,0:T(8,128)(2,1)} %collective-permute-done.20), channel_id=1, source_target_pairs={{1,0},{2,1},{3,2},{4,3},{5,4},{6,5},{7,6},{8,7},{9,8},{10,9},{11,1... | collective-permute-start | bytes 1572872 | tf_op jit(solution)/shard_map/ppermute | solution.py:17
  66.0 2.4 %collective-permute-start.25 = (bf16[8,256,128]{2,1,0:T(8,128)(2,1)}, bf16[8,256,128]{2,1,0:T(8,128)(2,1)S(1)}, u32[]{:S(2)}, u32[]{:S(2)}) collective-permute-start(bf16[8,256,128]{2,1,0:T(8,128)(2,1)} %collective-permute-done.22), channel_id=1, source_target_pairs={{1,0},{2,1},{3,2},{4,3},{5,4},{6,5},{7,6},{8,7},{9,8},{10,9},{11,1... | collective-permute-start | bytes 1572872 | tf_op jit(solution)/shard_map/ppermute | solution.py:17
  75.2 5.8 %collective-permute-start.26 = (bf16[8,256,128]{2,1,0:T(8,128)(2,1)S(1)}, bf16[8,256,128]{2,1,0:T(8,128)(2,1)S(1)}, u32[]{:S(2)}, u32[]{:S(2)}) collective-permute-start(bf16[8,256,128]{2,1,0:T(8,128)(2,1)S(1)} %collective-permute-done.23), channel_id=1, source_target_pairs={{1,0},{2,1},{3,2},{4,3},{5,4},{6,5},{7,6},{8,7},{9,8},{10,9},{11,1... | collective-permute-start | bytes 1572872 | tf_op jit(solution)/shard_map/ppermute | solution.py:17
  81.0 3.5 %collective-permute-start.28 = (bf16[8,256,128]{2,1,0:T(8,128)(2,1)S(1)}, bf16[8,256,128]{2,1,0:T(8,128)(2,1)S(1)}, u32[]{:S(2)}, u32[]{:S(2)}) collective-permute-start(bf16[8,256,128]{2,1,0:T(8,128)(2,1)S(1)} %collective-permute-done.25), channel_id=1, source_target_pairs={{1,0},{2,1},{3,2},{4,3},{5,4},{6,5},{7,6},{8,7},{9,8},{10,9},{11,1... | collective-permute-start | bytes 1572872 | tf_op jit(solution)/shard_map/ppermute | solution.py:17
  90.7 5.8 %collective-permute-start.29 = (bf16[8,256,128]{2,1,0:T(8,128)(2,1)S(1)}, bf16[8,256,128]{2,1,0:T(8,128)(2,1)}, u32[]{:S(2)}, u32[]{:S(2)}) collective-permute-start(bf16[8,256,128]{2,1,0:T(8,128)(2,1)S(1)} %collective-permute-done.26), channel_id=1, source_target_pairs={{1,0},{2,1},{3,2},{4,3},{5,4},{6,5},{7,6},{8,7},{9,8},{10,9},{11,1... | collective-permute-start | bytes 1572872 | tf_op jit(solution)/shard_map/ppermute | solution.py:17
  96.4 2.7 %collective-permute-start.31 = (bf16[8,256,128]{2,1,0:T(8,128)(2,1)S(1)}, bf16[8,256,128]{2,1,0:T(8,128)(2,1)}, u32[]{:S(2)}, u32[]{:S(2)}) collective-permute-start(bf16[8,256,128]{2,1,0:T(8,128)(2,1)S(1)} %collective-permute-done.28), channel_id=1, source_target_pairs={{1,0},{2,1},{3,2},{4,3},{5,4},{6,5},{7,6},{8,7},{9,8},{10,9},{11,1... | collective-permute-start | bytes 1572872 | tf_op jit(solution)/shard_map/ppermute | solution.py:17
  106.5 5.8 %collective-permute-start.32 = (bf16[8,256,128]{2,1,0:T(8,128)(2,1)}, bf16[8,256,128]{2,1,0:T(8,128)(2,1)}, u32[]{:S(2)}, u32[]{:S(2)}) collective-permute-start(bf16[8,256,128]{2,1,0:T(8,128)(2,1)} %collective-permute-done.29), channel_id=1, source_target_pairs={{1,0},{2,1},{3,2},{4,3},{5,4},{6,5},{7,6},{8,7},{9,8},{10,9},{11,1... | collective-permute-start | bytes 1572872 | tf_op jit(solution)/shard_map/ppermute | solution.py:17
  112.2 2.7 %collective-permute-start.34 = (bf16[8,256,128]{2,1,0:T(8,128)(2,1)}, bf16[8,256,128]{2,1,0:T(8,128)(2,1)}, u32[]{:S(2)}, u32[]{:S(2)}) collective-permute-start(bf16[8,256,128]{2,1,0:T(8,128)(2,1)} %collective-permute-done.31), channel_id=1, source_target_pairs={{1,0},{2,1},{3,2},{4,3},{5,4},{6,5},{7,6},{8,7},{9,8},{10,9},{11,1... | collective-permute-start | bytes 1572872 | tf_op jit(solution)/shard_map/ppermute | solution.py:17
  142.5 4.4 %collective-permute-start.24 = (f32[8,512]{1,0:T(8,128)S(1)}, f32[8,512]{1,0:T(8,128)S(1)}, u32[]{:S(2)}, u32[]{:S(2)}) collective-permute-start(f32[8,512]{1,0:T(8,128)S(1)} %pad_maximum_fusion), channel_id=1, source_target_pairs={{4,0},{5,1},{6,2},{7,3},{8,4},{9,5},{10,6},{11,7},{12,8},{13,9},{1... | collective-permute-start | bytes 49160 | tf_op jit(solution)/shard_map/ppermute | solution.py:17
  146.9 21.4 %collective-permute-start.27 = (f32[8,512]{1,0:T(8,128)S(1)}, f32[8,512]{1,0:T(8,128)S(1)}, u32[]{:S(2)}, u32[]{:S(2)}) collective-permute-start(f32[8,512]{1,0:T(8,128)S(1)} %pad_maximum_fusion), channel_id=1, source_target_pairs={{5,0},{6,1},{7,2},{8,3},{9,4},{10,5},{11,6},{12,7},{13,8},{14,9},{... | collective-permute-start | bytes 49160 | tf_op jit(solution)/shard_map/ppermute | solution.py:17
  172.7 3.0 %collective-permute-done.30 = f32[8,512]{1,0:T(8,128)S(1)} collective-permute-done((f32[8,512]{1,0:T(8,128)S(1)}, f32[8,512]{1,0:T(8,128)S(1)}, u32[]{:S(2)}, u32[]{:S(2)}) %collective-permute-start.30) | collective-permute-done | bytes 16416 | tf_op jit(solution)/shard_map/ppermute | solution.py:17
  175.8 2.8 %fusion.1 = (bf16[8,256,256]{1,2,0:T(8,128)(2,1)}, f32[8,256,256]{1,2,0:T(8,128)S(1)}) fusion(f32[8,256]{1,0:T(8,128)S(1)} %get-tuple-element.60, pred[256,256]{0,1:T(8,128)(4,1)S(1)} %copy-done.38, bf16[8,256,128]{2,1,0:T(8,128)(2,1)} %collective-permute-done.14, bf16[256,8,128]{2,0,1:T(8,128)(2,1)S(1)} %copy-done.10), kind=kOutput, calls=%fused_computation.40 | convolution fusion | flops 136839168 | bytes 4268032 | tf_op jit(solution)/shard_map/hkd,hqd->hkq/dot_general | solution.py:121
  180.5 2.8 %fusion.71 = (bf16[8,256,256]{1,2,0:T(8,128)(2,1)}, f32[8,256,256]{1,2,0:T(8,128)S(1)}) fusion(f32[8,256]{1,0:T(8,128)S(1)} %get-tuple-element.58, bf16[8,256,128]{2,1,0:T(8,128)(2,1)} %collective-permute-done.17, bf16[256,8,128]{2,0,1:T(8,128)(2,1)S(1)} %copy-done.10, pred[256,256]{0,1:T(8,128)(4,1)S(1)} %copy-done.37), kind=kOutput, calls=%fused_computation.175 | convolution fusion | flops 136839168 | bytes 4268032 | tf_op jit(solution)/shard_map/hkd,hqd->hkq/dot_general | solution.py:121
  184.8 2.8 %fusion.72 = (bf16[8,256,256]{1,2,0:T(8,128)(2,1)}, f32[8,256,256]{1,2,0:T(8,128)S(1)}) fusion(f32[8,256]{1,0:T(8,128)S(1)} %get-tuple-element.56, bf16[8,256,128]{2,1,0:T(8,128)(2,1)} %collective-permute-done.20, bf16[256,8,128]{2,0,1:T(8,128)(2,1)S(1)} %copy-done.10, pred[256,256]{0,1:T(8,128)(4,1)S(1)} %copy-done.36), kind=kOutput, calls=%fused_computation.176 | convolution fusion | flops 136839168 | bytes 4268032 | tf_op jit(solution)/shard_map/hkd,hqd->hkq/dot_general | solution.py:121
  194.6 2.8 %fusion.75 = (bf16[8,256,256]{1,2,0:T(8,128)(2,1)}, f32[8,256,256]{1,2,0:T(8,128)S(1)}) fusion(f32[8,256]{1,0:T(8,128)S(1)} %get-tuple-element.50, bf16[8,256,128]{2,1,0:T(8,128)(2,1)} %collective-permute-done.29, bf16[256,8,128]{2,0,1:T(8,128)(2,1)S(1)} %copy-done.10, pred[256,256]{0,1:T(8,128)(4,1)S(1)} %copy-done.33), kind=kOutput, calls=%fused_computation.179 | convolution fusion | flops 136839168 | bytes 4268032 | tf_op jit(solution)/shard_map/hkd,hqd->hkq/dot_general | solution.py:121
  198.9 2.7 %fusion.76 = (bf16[8,256,256]{1,2,0:T(8,128)(2,1)}, f32[8,256,256]{1,2,0:T(8,128)S(1)}) fusion(f32[8,256]{1,0:T(8,128)S(1)} %get-tuple-element.48, bf16[8,256,128]{2,1,0:T(8,128)(2,1)} %collective-permute-done.32, bf16[256,8,128]{2,0,1:T(8,128)(2,1)S(1)} %copy-done.10, pred[256,256]{0,1:T(8,128)(4,1)S(1)} %copy-done.32), kind=kOutput, calls=%fused_computation.180 | convolution fusion | flops 136839168 | bytes 4268032 | tf_op jit(solution)/shard_map/hkd,hqd->hkq/dot_general | solution.py:121
  (231 shorter events, 112.7 us)
Async XLA Ops:
  2.3 20.2 %collective-permute-start = (bf16[8,256,128]{2,1,0:T(8,128)(2,1)S(1)}, bf16[8,256,128]{2,1,0:T(8,128)(2,1)}, u32[]{:S(2)}, u32[]{:S(2)}) collective-permute-start(bf16[8,256,128]{2,1,0:T(8,128)(2,1)S(1)} %bitcast.241), channel_id=1, source_target_pairs={{0,1},{1,2},{2,3},{3,4},{4,5},{5,6},{6,7},{7,8},{8,9},{9,10},{10,1... | collective-permute-start | bytes 1572872 | tf_op jit(solution)/shard_map/ppermute | solution.py:17
  4.7 21.2 %collective-permute-start.7 = (bf16[8,256,128]{2,1,0:T(8,128)(2,1)S(1)}, bf16[8,256,128]{2,1,0:T(8,128)(2,1)}, u32[]{:S(2)}, u32[]{:S(2)}) collective-permute-start(bf16[8,256,128]{2,1,0:T(8,128)(2,1)S(1)} %bitcast.234), channel_id=1, source_target_pairs={{0,1},{1,2},{2,3},{3,4},{4,5},{5,6},{6,7},{7,8},{8,9},{9,10},{10,1... | collective-permute-start | bytes 1572872 | tf_op jit(solution)/shard_map/ppermute | solution.py:17
  9.8 18.1 %collective-permute-start.14 = (bf16[8,256,128]{2,1,0:T(8,128)(2,1)S(1)}, bf16[8,256,128]{2,1,0:T(8,128)(2,1)}, u32[]{:S(2)}, u32[]{:S(2)}) collective-permute-start(bf16[8,256,128]{2,1,0:T(8,128)(2,1)S(1)} %bitcast.233), channel_id=1, source_target_pairs={{1,0},{2,1},{3,2},{4,3},{5,4},{6,5},{7,6},{8,7},{9,8},{10,9},{11,1... | collective-permute-start | bytes 1572872 | tf_op jit(solution)/shard_map/ppermute | solution.py:17
  16.5 17.2 %collective-permute-start.16 = (bf16[8,256,128]{2,1,0:T(8,128)(2,1)S(1)}, bf16[8,256,128]{2,1,0:T(8,128)(2,1)}, u32[]{:S(2)}, u32[]{:S(2)}) collective-permute-start(bf16[8,256,128]{2,1,0:T(8,128)(2,1)S(1)} %bitcast.232), channel_id=1, source_target_pairs={{1,0},{2,1},{3,2},{4,3},{5,4},{6,5},{7,6},{8,7},{9,8},{10,9},{11,1... | collective-permute-start | bytes 1572872 | tf_op jit(solution)/shard_map/ppermute | solution.py:17
  36.6 18.2 %collective-permute-start.2 = (bf16[8,256,128]{2,1,0:T(8,128)(2,1)}, bf16[8,256,128]{2,1,0:T(8,128)(2,1)}, u32[]{:S(2)}, u32[]{:S(2)}) collective-permute-start(bf16[8,256,128]{2,1,0:T(8,128)(2,1)} %collective-permute-done.1), channel_id=1, source_target_pairs={{0,1},{1,2},{2,3},{3,4},{4,5},{5,6},{6,7},{7,8},{8,9},{9,10},{10,1... | collective-permute-start | bytes 1572872 | tf_op jit(solution)/shard_map/ppermute | solution.py:17
  41.1 17.3 %collective-permute-start.9 = (bf16[8,256,128]{2,1,0:T(8,128)(2,1)}, bf16[8,256,128]{2,1,0:T(8,128)(2,1)}, u32[]{:S(2)}, u32[]{:S(2)}) collective-permute-start(bf16[8,256,128]{2,1,0:T(8,128)(2,1)} %collective-permute-done.8), channel_id=1, source_target_pairs={{0,1},{1,2},{2,3},{3,4},{4,5},{5,6},{6,7},{7,8},{8,9},{9,10},{10,1... | collective-permute-start | bytes 1572872 | tf_op jit(solution)/shard_map/ppermute | solution.py:17
  43.0 17.3 %collective-permute-start.20 = (bf16[8,256,128]{2,1,0:T(8,128)(2,1)}, bf16[8,256,128]{2,1,0:T(8,128)(2,1)}, u32[]{:S(2)}, u32[]{:S(2)}) collective-permute-start(bf16[8,256,128]{2,1,0:T(8,128)(2,1)} %collective-permute-done.17), channel_id=1, source_target_pairs={{1,0},{2,1},{3,2},{4,3},{5,4},{6,5},{7,6},{8,7},{9,8},{10,9},{11,1... | collective-permute-start | bytes 1572872 | tf_op jit(solution)/shard_map/ppermute | solution.py:17
  48.8 17.3 %collective-permute-start.22 = (bf16[8,256,128]{2,1,0:T(8,128)(2,1)}, bf16[8,256,128]{2,1,0:T(8,128)(2,1)}, u32[]{:S(2)}, u32[]{:S(2)}) collective-permute-start(bf16[8,256,128]{2,1,0:T(8,128)(2,1)} %collective-permute-done.19), channel_id=1, source_target_pairs={{1,0},{2,1},{3,2},{4,3},{5,4},{6,5},{7,6},{8,7},{9,8},{10,9},{11,1... | collective-permute-start | bytes 1572872 | tf_op jit(solution)/shard_map/ppermute | solution.py:17
  70.3 16.0 %collective-permute-start.4 = (bf16[8,256,128]{2,1,0:T(8,128)(2,1)S(1)}, bf16[8,256,128]{2,1,0:T(8,128)(2,1)S(1)}, u32[]{:S(2)}, u32[]{:S(2)}) collective-permute-start(bf16[8,256,128]{2,1,0:T(8,128)(2,1)S(1)} %collective-permute-done.3), channel_id=1, source_target_pairs={{0,1},{1,2},{2,3},{3,4},{4,5},{5,6},{6,7},{7,8},{8,9},{9,10},{10,1... | collective-permute-start | bytes 1572872 | tf_op jit(solution)/shard_map/ppermute | solution.py:17
  75.2 15.5 %collective-permute-start.26 = (bf16[8,256,128]{2,1,0:T(8,128)(2,1)S(1)}, bf16[8,256,128]{2,1,0:T(8,128)(2,1)S(1)}, u32[]{:S(2)}, u32[]{:S(2)}) collective-permute-start(bf16[8,256,128]{2,1,0:T(8,128)(2,1)S(1)} %collective-permute-done.23), channel_id=1, source_target_pairs={{1,0},{2,1},{3,2},{4,3},{5,4},{6,5},{7,6},{8,7},{9,8},{10,9},{11,1... | collective-permute-start | bytes 1572872 | tf_op jit(solution)/shard_map/ppermute | solution.py:17
  81.0 15.5 %collective-permute-start.28 = (bf16[8,256,128]{2,1,0:T(8,128)(2,1)S(1)}, bf16[8,256,128]{2,1,0:T(8,128)(2,1)S(1)}, u32[]{:S(2)}, u32[]{:S(2)}) collective-permute-start(bf16[8,256,128]{2,1,0:T(8,128)(2,1)S(1)} %collective-permute-done.25), channel_id=1, source_target_pairs={{1,0},{2,1},{3,2},{4,3},{5,4},{6,5},{7,6},{8,7},{9,8},{10,9},{11,1... | collective-permute-start | bytes 1572872 | tf_op jit(solution)/shard_map/ppermute | solution.py:17
  88.7 15.8 %collective-permute-start.12 = (bf16[8,256,128]{2,1,0:T(8,128)(2,1)S(1)}, bf16[8,256,128]{2,1,0:T(8,128)(2,1)S(1)}, u32[]{:S(2)}, u32[]{:S(2)}) collective-permute-start(bf16[8,256,128]{2,1,0:T(8,128)(2,1)S(1)} %collective-permute-done.11), channel_id=1, source_target_pairs={{0,1},{1,2},{2,3},{3,4},{4,5},{5,6},{6,7},{7,8},{8,9},{9,10},{10,1... | collective-permute-start | bytes 1572872 | tf_op jit(solution)/shard_map/ppermute | solution.py:17
  90.7 15.8 %collective-permute-start.29 = (bf16[8,256,128]{2,1,0:T(8,128)(2,1)S(1)}, bf16[8,256,128]{2,1,0:T(8,128)(2,1)}, u32[]{:S(2)}, u32[]{:S(2)}) collective-permute-start(bf16[8,256,128]{2,1,0:T(8,128)(2,1)S(1)} %collective-permute-done.26), channel_id=1, source_target_pairs={{1,0},{2,1},{3,2},{4,3},{5,4},{6,5},{7,6},{8,7},{9,8},{10,9},{11,1... | collective-permute-start | bytes 1572872 | tf_op jit(solution)/shard_map/ppermute | solution.py:17
  96.4 15.8 %collective-permute-start.31 = (bf16[8,256,128]{2,1,0:T(8,128)(2,1)S(1)}, bf16[8,256,128]{2,1,0:T(8,128)(2,1)}, u32[]{:S(2)}, u32[]{:S(2)}) collective-permute-start(bf16[8,256,128]{2,1,0:T(8,128)(2,1)S(1)} %collective-permute-done.28), channel_id=1, source_target_pairs={{1,0},{2,1},{3,2},{4,3},{5,4},{6,5},{7,6},{8,7},{9,8},{10,9},{11,1... | collective-permute-start | bytes 1572872 | tf_op jit(solution)/shard_map/ppermute | solution.py:17
  100.0 15.7 %collective-permute-start.6 = (bf16[8,256,128]{2,1,0:T(8,128)(2,1)S(1)}, bf16[8,256,128]{2,1,0:T(8,128)(2,1)S(1)}, u32[]{:S(2)}, u32[]{:S(2)}) collective-permute-start(bf16[8,256,128]{2,1,0:T(8,128)(2,1)S(1)} %collective-permute-done.5), channel_id=1, source_target_pairs={{0,1},{1,2},{2,3},{3,4},{4,5},{5,6},{6,7},{7,8},{8,9},{9,10},{10,1... | collective-permute-start | bytes 1572872 | tf_op jit(solution)/shard_map/ppermute | solution.py:17
  104.5 24.7 %collective-permute-start.13 = (bf16[8,256,128]{2,1,0:T(8,128)(2,1)S(1)}, bf16[8,256,128]{2,1,0:T(8,128)(2,1)S(1)}, u32[]{:S(2)}, u32[]{:S(2)}) collective-permute-start(bf16[8,256,128]{2,1,0:T(8,128)(2,1)S(1)} %collective-permute-done.12), channel_id=1, source_target_pairs={{0,1},{1,2},{2,3},{3,4},{4,5},{5,6},{6,7},{7,8},{8,9},{9,10},{10,1... | collective-permute-start | bytes 1572872 | tf_op jit(solution)/shard_map/ppermute | solution.py:17
  106.5 92.4 %collective-permute-start.32 = (bf16[8,256,128]{2,1,0:T(8,128)(2,1)}, bf16[8,256,128]{2,1,0:T(8,128)(2,1)}, u32[]{:S(2)}, u32[]{:S(2)}) collective-permute-start(bf16[8,256,128]{2,1,0:T(8,128)(2,1)} %collective-permute-done.29), channel_id=1, source_target_pairs={{1,0},{2,1},{3,2},{4,3},{5,4},{6,5},{7,6},{8,7},{9,8},{10,9},{11,1... | collective-permute-start | bytes 1572872 | tf_op jit(solution)/shard_map/ppermute | solution.py:17
  112.2 89.4 %collective-permute-start.34 = (bf16[8,256,128]{2,1,0:T(8,128)(2,1)}, bf16[8,256,128]{2,1,0:T(8,128)(2,1)}, u32[]{:S(2)}, u32[]{:S(2)}) collective-permute-start(bf16[8,256,128]{2,1,0:T(8,128)(2,1)} %collective-permute-done.31), channel_id=1, source_target_pairs={{1,0},{2,1},{3,2},{4,3},{5,4},{6,5},{7,6},{8,7},{9,8},{10,9},{11,1... | collective-permute-start | bytes 1572872 | tf_op jit(solution)/shard_map/ppermute | solution.py:17
  118.2 24.3 %collective-permute-start.15 = (f32[8,512]{1,0:T(8,128)S(1)}, f32[8,512]{1,0:T(8,128)S(1)}, u32[]{:S(2)}, u32[]{:S(2)}) collective-permute-start(f32[8,512]{1,0:T(8,128)S(1)} %pad_maximum_fusion), channel_id=1, source_target_pairs={{1,0},{2,1},{3,2},{4,3},{5,4},{6,5},{7,6},{8,7},{9,8},{10,9},{11,1... | collective-permute-start | bytes 49160 | tf_op jit(solution)/shard_map/ppermute | solution.py:17
  120.1 26.7 %collective-permute-start.18 = (f32[8,512]{1,0:T(8,128)S(1)}, f32[8,512]{1,0:T(8,128)S(1)}, u32[]{:S(2)}, u32[]{:S(2)}) collective-permute-start(f32[8,512]{1,0:T(8,128)S(1)} %pad_maximum_fusion), channel_id=1, source_target_pairs={{2,0},{3,1},{4,2},{5,3},{6,4},{7,5},{8,6},{9,7},{10,8},{11,9},{12,... | collective-permute-start | bytes 49160 | tf_op jit(solution)/shard_map/ppermute | solution.py:17
  129.3 39.0 %collective-permute-start.21 = (f32[8,512]{1,0:T(8,128)S(1)}, f32[8,512]{1,0:T(8,128)S(1)}, u32[]{:S(2)}, u32[]{:S(2)}) collective-permute-start(f32[8,512]{1,0:T(8,128)S(1)} %pad_maximum_fusion), channel_id=1, source_target_pairs={{3,0},{4,1},{5,2},{6,3},{7,4},{8,5},{9,6},{10,7},{11,8},{12,9},{13... | collective-permute-start | bytes 49160 | tf_op jit(solution)/shard_map/ppermute | solution.py:17
  142.5 28.0 %collective-permute-start.24 = (f32[8,512]{1,0:T(8,128)S(1)}, f32[8,512]{1,0:T(8,128)S(1)}, u32[]{:S(2)}, u32[]{:S(2)}) collective-permute-start(f32[8,512]{1,0:T(8,128)S(1)} %pad_maximum_fusion), channel_id=1, source_target_pairs={{4,0},{5,1},{6,2},{7,3},{8,4},{9,5},{10,6},{11,7},{12,8},{13,9},{1... | collective-permute-start | bytes 49160 | tf_op jit(solution)/shard_map/ppermute | solution.py:17
  146.9 25.8 %collective-permute-start.27 = (f32[8,512]{1,0:T(8,128)S(1)}, f32[8,512]{1,0:T(8,128)S(1)}, u32[]{:S(2)}, u32[]{:S(2)}) collective-permute-start(f32[8,512]{1,0:T(8,128)S(1)} %pad_maximum_fusion), channel_id=1, source_target_pairs={{5,0},{6,1},{7,2},{8,3},{9,4},{10,5},{11,6},{12,7},{13,8},{14,9},{... | collective-permute-start | bytes 49160 | tf_op jit(solution)/shard_map/ppermute | solution.py:17
  170.5 28.3 %collective-permute-start.33 = (f32[8,512]{1,0:T(8,128)S(1)}, f32[8,512]{1,0:T(8,128)S(1)}, u32[]{:S(2)}, u32[]{:S(2)}) collective-permute-start(f32[8,512]{1,0:T(8,128)S(1)} %pad_maximum_fusion), channel_id=1, source_target_pairs={{7,0},{8,1},{9,2},{10,3},{11,4},{12,5},{13,6},{14,7},{15,8},{16,9}... | collective-permute-start | bytes 49160 | tf_op jit(solution)/shard_map/ppermute | solution.py:17
  (51 other events, 394.5 us)
where the time goes:
time: 226 us; the launch traced here: 223 us
  starting transfers between devices  124 us (55%)
  matrix products  65.1 us (29%)
  local copies, waits for them, and re-layouts  16.3 us (7%)
  waiting for transfers between devices  8.61 us (4%)
  other arithmetic  6.75 us (3%)
    ppermute x35, starting transfers between devices, from_behind(): lax.ppermute(value, axis, [(source, source + steps) for source in range(f...  124 us
    dot_general x7, matrix products, key_tile(): jnp.einsum('hkd,hqd->hkq', key_h, q_in, preferred_element_type=jnp.float32)  17.3 us
    unnamed x88, local copies, waits for them, and re-layouts  13 us
    dot_general x7, matrix products, key_tile(): jnp.einsum('hkd,hqd->hkq', value_h, g_in, preferred_element_type=jnp.floa...  8.89 us
    ppermute x35, waiting for transfers between devices, from_behind(): lax.ppermute(value, axis, [(source, source + steps) for source in range(f...  8.61 us
    dot_general x8, matrix products, tile_grads(): dprob = jnp.einsum('hqd,hkd->hqk', g, v, preferred_element_type=jnp.float32)  8.43 us
    dot_general x7, matrix products, key_tile(): jnp.einsum('hkq,hqd->hkd', prob_b, g_in, preferred_element_type=jnp.float32)  8.05 us
    dot_general x7, matrix products, key_tile(): jnp.einsum('hkq,hqd->hkd', dscore, q_in, preferred_element_type=jnp.float32)  7.81 us
  transfers between devices with their start and end apart: 35, of which 4 were waited for; matrix products, arithmetic and copies ran while one was open for 28% of the time, Pallas kernels for 0%

commit v1 on v0

--- a/solution.py
+++ b/solution.py
@@ -59,15 +59,21 @@
         "hqd,hqd->hq", grad_h, to_heads(forward_out), preferred_element_type=jnp.float32
     )
 
-    key_values = [(key_h, value_h)]
+    keys_in = [key_h]
     query_grads = [(query_h, grad_h)]
-    moving_kv = (key_h, value_h)
+    moving_k = key_h
     moving_qg = (query_h, grad_h)
     for step in range(1, window):
-        moving_kv = from_behind(moving_kv, axes, 1)
+        moving_k = from_behind(moving_k, axes, 1)
         moving_qg = from_behind(moving_qg, axes, -1)
-        key_values.append(moving_kv)
+        keys_in.append(moving_k)
         query_grads.append(moving_qg)
+    values_in = [value_h]
+    moving_v, _ = lax.optimization_barrier((value_h, moving_k))
+    for step in range(1, window):
+        moving_v = from_behind(moving_v, axes, 1)
+        values_in.append(moving_v)
+    key_values = list(zip(keys_in, values_in))
 
     def scores_of(q, k, mask):
         s = jnp.einsum("hqd,hkd->hqk", q, k, preferred_element_type=jnp.float32) * scale
@@ -79,7 +85,7 @@
         return (top, jnp.sum(jnp.exp(s - top[..., None]), axis=2))
 
     def merged(step, stats):
-        part = tile_stats(query_h, key_values[step][0], query_masks[step])
+        part = tile_stats(query_h, keys_in[step], query_masks[step])
         top = jnp.maximum(stats[0], part[0])
         total = stats[1] * jnp.exp(stats[0] - top) + part[1] * jnp.exp(part[0] - top)
         return (top, total)

time: 226 us -> 286 us (1.27)
  the two profiles are of different devices: /device:TPU:14 before, /device:TPU:6 now
where the time goes in v1:
time: 286 us; the launch traced here: 283 us
  starting transfers between devices  127 us (44%)
  waiting for transfers between devices  70 us (24%)
  matrix products  56.2 us (20%)
  local copies, waits for them, and re-layouts  21.3 us (7%)
  other arithmetic  6.74 us (2%)
    ppermute x35, starting transfers between devices, from_behind(): lax.ppermute(value, axis, [(source, source + steps) for source in range(f...  127 us
    ppermute x35, waiting for transfers between devices, from_behind(): lax.ppermute(value, axis, [(source, source + steps) for source in range(f...  70 us
    unnamed x134, local copies, waits for them, and re-layouts  16.2 us
    dot_general x7, matrix products, key_tile(): jnp.einsum('hkd,hqd->hkq', key_h, q_in, preferred_element_type=jnp.float32)  15.2 us
    dot_general x7, matrix products, key_tile(): jnp.einsum('hkq,hqd->hkd', prob_b, g_in, preferred_element_type=jnp.float32)  7.24 us
    dot_general x8, matrix products, scores_of(): jnp.einsum('hqd,hkd->hqk', q, k, preferred_element_type=jnp.float32) * scale  6.95 us
    dot_general x7, matrix products, key_tile(): jnp.einsum('hkd,hqd->hkq', value_h, g_in, preferred_element_type=jnp.floa...  6.65 us
    dot_general x8, matrix products, tile_grads(): dprob = jnp.einsum('hqd,hkd->hqk', g, v, preferred_element_type=jnp.float32)  6.25 us
  transfers between devices with their start and end apart: 35, of which 13 were waited for; matrix products, arithmetic and copies ran while one was open for 26% of the time, Pallas kernels for 0%

profile of v1, /device:TPU:6, one launch (start us, length us, event | category | flops | bytes accessed | tf_op | source)
XLA Modules:
  0.0 283.3 jit_solution(18089689821887866847)
XLA Ops:
  4.9 9.9 %collective-permute-start.14 = (bf16[8,256,128]{2,1,0:T(8,128)(2,1)S(1)}, bf16[8,256,128]{2,1,0:T(8,128)(2,1)}, u32[]{:S(2)}, u32[]{:S(2)}) collective-permute-start(bf16[8,256,128]{2,1,0:T(8,128)(2,1)S(1)} %bitcast.261), channel_id=1, source_target_pairs={{1,0},{2,1},{3,2},{4,3},{5,4},{6,5},{7,6},{8,7},{9,8},{10,9},{11,1... | collective-permute-start | bytes 1572872 | tf_op jit(solution)/shard_map/ppermute | solution.py:17
  15.3 2.6 collective-permute-start.16
  24.8 7.9 %collective-permute-start.17 = (bf16[8,256,128]{2,1,0:T(8,128)(2,1)}, bf16[8,256,128]{2,1,0:T(8,128)(2,1)}, u32[]{:S(2)}, u32[]{:S(2)}) collective-permute-start(bf16[8,256,128]{2,1,0:T(8,128)(2,1)} %collective-permute-done.14), channel_id=1, source_target_pairs={{1,0},{2,1},{3,2},{4,3},{5,4},{6,5},{7,6},{8,7},{9,8},{10,9},{11,1... | collective-permute-start | bytes 1572872 | tf_op jit(solution)/shard_map/ppermute | solution.py:17
  32.7 2.5 collective-permute-start.19
  39.7 8.0 %collective-permute-start.20 = (bf16[8,256,128]{2,1,0:T(8,128)(2,1)}, bf16[8,256,128]{2,1,0:T(8,128)(2,1)}, u32[]{:S(2)}, u32[]{:S(2)}) collective-permute-start(bf16[8,256,128]{2,1,0:T(8,128)(2,1)} %collective-permute-done.17), channel_id=1, source_target_pairs={{1,0},{2,1},{3,2},{4,3},{5,4},{6,5},{7,6},{8,7},{9,8},{10,9},{11,1... | collective-permute-start | bytes 1572872 | tf_op jit(solution)/shard_map/ppermute | solution.py:17
  47.7 5.6 %collective-permute-start.22 = (bf16[8,256,128]{2,1,0:T(8,128)(2,1)}, bf16[8,256,128]{2,1,0:T(8,128)(2,1)}, u32[]{:S(2)}, u32[]{:S(2)}) collective-permute-start(bf16[8,256,128]{2,1,0:T(8,128)(2,1)} %collective-permute-done.19), channel_id=1, source_target_pairs={{1,0},{2,1},{3,2},{4,3},{5,4},{6,5},{7,6},{8,7},{9,8},{10,9},{11,1... | collective-permute-start | bytes 1572872 | tf_op jit(solution)/shard_map/ppermute | solution.py:17
  63.6 7.9 %collective-permute-start.23 = (bf16[8,256,128]{2,1,0:T(8,128)(2,1)}, bf16[8,256,128]{2,1,0:T(8,128)(2,1)S(1)}, u32[]{:S(2)}, u32[]{:S(2)}) collective-permute-start(bf16[8,256,128]{2,1,0:T(8,128)(2,1)} %collective-permute-done.20), channel_id=1, source_target_pairs={{1,0},{2,1},{3,2},{4,3},{5,4},{6,5},{7,6},{8,7},{9,8},{10,9},{11,1... | collective-permute-start | bytes 1572872 | tf_op jit(solution)/shard_map/ppermute | solution.py:17
  78.4 7.9 %collective-permute-start.26 = (bf16[8,256,128]{2,1,0:T(8,128)(2,1)S(1)}, bf16[8,256,128]{2,1,0:T(8,128)(2,1)S(1)}, u32[]{:S(2)}, u32[]{:S(2)}) collective-permute-start(bf16[8,256,128]{2,1,0:T(8,128)(2,1)S(1)} %collective-permute-done.23), channel_id=1, source_target_pairs={{1,0},{2,1},{3,2},{4,3},{5,4},{6,5},{7,6},{8,7},{9,8},{10,9},{11,1... | collective-permute-start | bytes 1572872 | tf_op jit(solution)/shard_map/ppermute | solution.py:17
  86.4 5.6 %collective-permute-start.28 = (bf16[8,256,128]{2,1,0:T(8,128)(2,1)S(1)}, bf16[8,256,128]{2,1,0:T(8,128)(2,1)S(1)}, u32[]{:S(2)}, u32[]{:S(2)}) collective-permute-start(bf16[8,256,128]{2,1,0:T(8,128)(2,1)S(1)} %collective-permute-done.25), channel_id=1, source_target_pairs={{1,0},{2,1},{3,2},{4,3},{5,4},{6,5},{7,6},{8,7},{9,8},{10,9},{11,1... | collective-permute-start | bytes 1572872 | tf_op jit(solution)/shard_map/ppermute | solution.py:17
  96.3 7.9 %collective-permute-start.29 = (bf16[8,256,128]{2,1,0:T(8,128)(2,1)S(1)}, bf16[8,256,128]{2,1,0:T(8,128)(2,1)S(1)}, u32[]{:S(2)}, u32[]{:S(2)}) collective-permute-start(bf16[8,256,128]{2,1,0:T(8,128)(2,1)S(1)} %collective-permute-done.26), channel_id=1, source_target_pairs={{1,0},{2,1},{3,2},{4,3},{5,4},{6,5},{7,6},{8,7},{9,8},{10,9},{11,1... | collective-permute-start | bytes 1572872 | tf_op jit(solution)/shard_map/ppermute | solution.py:17
  104.2 2.5 collective-permute-start.31
  110.8 8.0 %collective-permute-start.32 = (bf16[8,256,128]{2,1,0:T(8,128)(2,1)S(1)}, bf16[8,256,128]{2,1,0:T(8,128)(2,1)S(1)}, u32[]{:S(2)}, u32[]{:S(2)}) collective-permute-start(bf16[8,256,128]{2,1,0:T(8,128)(2,1)S(1)} %collective-permute-done.29), channel_id=1, source_target_pairs={{1,0},{2,1},{3,2},{4,3},{5,4},{6,5},{7,6},{8,7},{9,8},{10,9},{11,1... | collective-permute-start | bytes 1572872 | tf_op jit(solution)/shard_map/ppermute | solution.py:17
  118.9 5.8 %collective-permute-start.34 = (bf16[8,256,128]{2,1,0:T(8,128)(2,1)S(1)}, bf16[8,256,128]{2,1,0:T(8,128)(2,1)S(1)}, u32[]{:S(2)}, u32[]{:S(2)}) collective-permute-start(bf16[8,256,128]{2,1,0:T(8,128)(2,1)S(1)} %collective-permute-done.31), channel_id=1, source_target_pairs={{1,0},{2,1},{3,2},{4,3},{5,4},{6,5},{7,6},{8,7},{9,8},{10,9},{11,1... | collective-permute-start | bytes 1572872 | tf_op jit(solution)/shard_map/ppermute | solution.py:17
  146.6 3.1 %collective-permute-start.7 = (bf16[8,256,128]{2,1,0:T(8,128)(2,1)S(1)}, bf16[8,256,128]{2,1,0:T(8,128)(2,1)}, u32[]{:S(2)}, u32[]{:S(2)}) collective-permute-start(bf16[8,256,128]{2,1,0:T(8,128)(2,1)S(1)} %bitcast.262), channel_id=1, source_target_pairs={{0,1},{1,2},{2,3},{3,4},{4,5},{5,6},{6,7},{7,8},{8,9},{9,10},{10,1... | collective-permute-start | bytes 1572872 | tf_op jit(solution)/shard_map/ppermute | solution.py:17
  149.9 2.7 fusion.8
  154.6 2.8 fusion.78
  158.9 2.8 fusion.79
  192.6 2.7 collective-permute-start.8
  198.6 9.1 %collective-permute-done.8 = bf16[8,256,128]{2,1,0:T(8,128)(2,1)S(1)} collective-permute-done((bf16[8,256,128]{2,1,0:T(8,128)(2,1)}, bf16[8,256,128]{2,1,0:T(8,128)(2,1)S(1)}, u32[]{:S(2)}, u32[]{:S(2)}) %collective-permute-start.8) | collective-permute-done | bytes 524320 | tf_op jit(solution)/shard_map/ppermute | solution.py:17
  211.8 10.5 %collective-permute-done.9 = bf16[8,256,128]{2,1,0:T(8,128)(2,1)S(1)} collective-permute-done((bf16[8,256,128]{2,1,0:T(8,128)(2,1)S(1)}, bf16[8,256,128]{2,1,0:T(8,128)(2,1)S(1)}, u32[]{:S(2)}, u32[]{:S(2)}) %collective-permute-start.9) | collective-permute-done | bytes 524320 | tf_op jit(solution)/shard_map/ppermute | solution.py:17
  226.6 10.5 %collective-permute-done.10 = bf16[8,256,128]{2,1,0:T(8,128)(2,1)S(1)} collective-permute-done((bf16[8,256,128]{2,1,0:T(8,128)(2,1)S(1)}, bf16[8,256,128]{2,1,0:T(8,128)(2,1)S(1)}, u32[]{:S(2)}, u32[]{:S(2)}) %collective-permute-start.10) | collective-permute-done | bytes 524320 | tf_op jit(solution)/shard_map/ppermute | solution.py:17
  240.1 11.7 %collective-permute-done.11 = bf16[8,256,128]{2,1,0:T(8,128)(2,1)S(1)} collective-permute-done((bf16[8,256,128]{2,1,0:T(8,128)(2,1)S(1)}, bf16[8,256,128]{2,1,0:T(8,128)(2,1)S(1)}, u32[]{:S(2)}, u32[]{:S(2)}) %collective-permute-start.11) | collective-permute-done | bytes 524320 | tf_op jit(solution)/shard_map/ppermute | solution.py:17
  254.8 11.7 %collective-permute-done.12 = bf16[8,256,128]{2,1,0:T(8,128)(2,1)S(1)} collective-permute-done((bf16[8,256,128]{2,1,0:T(8,128)(2,1)S(1)}, bf16[8,256,128]{2,1,0:T(8,128)(2,1)S(1)}, u32[]{:S(2)}, u32[]{:S(2)}) %collective-permute-start.12) | collective-permute-done | bytes 524320 | tf_op jit(solution)/shard_map/ppermute | solution.py:17
  269.5 11.7 %collective-permute-done.13 = bf16[8,256,128]{2,1,0:T(8,128)(2,1)S(1)} collective-permute-done((bf16[8,256,128]{2,1,0:T(8,128)(2,1)S(1)}, bf16[8,256,128]{2,1,0:T(8,128)(2,1)S(1)}, u32[]{:S(2)}, u32[]{:S(2)}) %collective-permute-start.13) | collective-permute-done | bytes 524320 | tf_op jit(solution)/shard_map/ppermute | solution.py:17
  (277 shorter events, 119.6 us)
Async XLA Ops:
  2.3 19.1 %collective-permute-start = (bf16[8,256,128]{2,1,0:T(8,128)(2,1)S(1)}, bf16[8,256,128]{2,1,0:T(8,128)(2,1)}, u32[]{:S(2)}, u32[]{:S(2)}) collective-permute-start(bf16[8,256,128]{2,1,0:T(8,128)(2,1)S(1)} %bitcast.269), channel_id=1, source_target_pairs={{0,1},{1,2},{2,3},{3,4},{4,5},{5,6},{6,7},{7,8},{8,9},{9,10},{10,1... | collective-permute-start | bytes 1572872 | tf_op jit(solution)/shard_map/ppermute | solution.py:17
  4.9 20.0 %collective-permute-start.14 = (bf16[8,256,128]{2,1,0:T(8,128)(2,1)S(1)}, bf16[8,256,128]{2,1,0:T(8,128)(2,1)}, u32[]{:S(2)}, u32[]{:S(2)}) collective-permute-start(bf16[8,256,128]{2,1,0:T(8,128)(2,1)S(1)} %bitcast.261), channel_id=1, source_target_pairs={{1,0},{2,1},{3,2},{4,3},{5,4},{6,5},{7,6},{8,7},{9,8},{10,9},{11,1... | collective-permute-start | bytes 1572872 | tf_op jit(solution)/shard_map/ppermute | solution.py:17
  15.3 17.4 %collective-permute-start.16 = (bf16[8,256,128]{2,1,0:T(8,128)(2,1)S(1)}, bf16[8,256,128]{2,1,0:T(8,128)(2,1)}, u32[]{:S(2)}, u32[]{:S(2)}) collective-permute-start(bf16[8,256,128]{2,1,0:T(8,128)(2,1)S(1)} %bitcast.260), channel_id=1, source_target_pairs={{1,0},{2,1},{3,2},{4,3},{5,4},{6,5},{7,6},{8,7},{9,8},{10,9},{11,1... | collective-permute-start | bytes 1572872 | tf_op jit(solution)/shard_map/ppermute | solution.py:17
  21.4 15.0 %collective-permute-start.1 = (bf16[8,256,128]{2,1,0:T(8,128)(2,1)}, bf16[8,256,128]{2,1,0:T(8,128)(2,1)}, u32[]{:S(2)}, u32[]{:S(2)}) collective-permute-start(bf16[8,256,128]{2,1,0:T(8,128)(2,1)} %collective-permute-done), channel_id=1, source_target_pairs={{0,1},{1,2},{2,3},{3,4},{4,5},{5,6},{6,7},{7,8},{8,9},{9,10},{10,1... | collective-permute-start | bytes 1572872 | tf_op jit(solution)/shard_map/ppermute | solution.py:17
  24.8 14.9 %collective-permute-start.17 = (bf16[8,256,128]{2,1,0:T(8,128)(2,1)}, bf16[8,256,128]{2,1,0:T(8,128)(2,1)}, u32[]{:S(2)}, u32[]{:S(2)}) collective-permute-start(bf16[8,256,128]{2,1,0:T(8,128)(2,1)} %collective-permute-done.14), channel_id=1, source_target_pairs={{1,0},{2,1},{3,2},{4,3},{5,4},{6,5},{7,6},{8,7},{9,8},{10,9},{11,1... | collective-permute-start | bytes 1572872 | tf_op jit(solution)/shard_map/ppermute | solution.py:17
  32.7 15.0 %collective-permute-start.19 = (bf16[8,256,128]{2,1,0:T(8,128)(2,1)}, bf16[8,256,128]{2,1,0:T(8,128)(2,1)}, u32[]{:S(2)}, u32[]{:S(2)}) collective-permute-start(bf16[8,256,128]{2,1,0:T(8,128)(2,1)} %collective-permute-done.16), channel_id=1, source_target_pairs={{1,0},{2,1},{3,2},{4,3},{5,4},{6,5},{7,6},{8,7},{9,8},{10,9},{11,1... | collective-permute-start | bytes 1572872 | tf_op jit(solution)/shard_map/ppermute | solution.py:17
  36.4 23.6 %collective-permute-start.2 = (bf16[8,256,128]{2,1,0:T(8,128)(2,1)}, bf16[8,256,128]{2,1,0:T(8,128)(2,1)}, u32[]{:S(2)}, u32[]{:S(2)}) collective-permute-start(bf16[8,256,128]{2,1,0:T(8,128)(2,1)} %collective-permute-done.1), channel_id=1, source_target_pairs={{0,1},{1,2},{2,3},{3,4},{4,5},{5,6},{6,7},{7,8},{8,9},{9,10},{10,1... | collective-permute-start | bytes 1572872 | tf_op jit(solution)/shard_map/ppermute | solution.py:17
  39.7 23.9 %collective-permute-start.20 = (bf16[8,256,128]{2,1,0:T(8,128)(2,1)}, bf16[8,256,128]{2,1,0:T(8,128)(2,1)}, u32[]{:S(2)}, u32[]{:S(2)}) collective-permute-start(bf16[8,256,128]{2,1,0:T(8,128)(2,1)} %collective-permute-done.17), channel_id=1, source_target_pairs={{1,0},{2,1},{3,2},{4,3},{5,4},{6,5},{7,6},{8,7},{9,8},{10,9},{11,1... | collective-permute-start | bytes 1572872 | tf_op jit(solution)/shard_map/ppermute | solution.py:17
  47.7 23.7 %collective-permute-start.22 = (bf16[8,256,128]{2,1,0:T(8,128)(2,1)}, bf16[8,256,128]{2,1,0:T(8,128)(2,1)}, u32[]{:S(2)}, u32[]{:S(2)}) collective-permute-start(bf16[8,256,128]{2,1,0:T(8,128)(2,1)} %collective-permute-done.19), channel_id=1, source_target_pairs={{1,0},{2,1},{3,2},{4,3},{5,4},{6,5},{7,6},{8,7},{9,8},{10,9},{11,1... | collective-permute-start | bytes 1572872 | tf_op jit(solution)/shard_map/ppermute | solution.py:17
  60.0 15.2 %collective-permute-start.3 = (bf16[8,256,128]{2,1,0:T(8,128)(2,1)}, bf16[8,256,128]{2,1,0:T(8,128)(2,1)S(1)}, u32[]{:S(2)}, u32[]{:S(2)}) collective-permute-start(bf16[8,256,128]{2,1,0:T(8,128)(2,1)} %collective-permute-done.2), channel_id=1, source_target_pairs={{0,1},{1,2},{2,3},{3,4},{4,5},{5,6},{6,7},{7,8},{8,9},{9,10},{10,1... | collective-permute-start | bytes 1572872 | tf_op jit(solution)/shard_map/ppermute | solution.py:17
  63.6 14.9 %collective-permute-start.23 = (bf16[8,256,128]{2,1,0:T(8,128)(2,1)}, bf16[8,256,128]{2,1,0:T(8,128)(2,1)S(1)}, u32[]{:S(2)}, u32[]{:S(2)}) collective-permute-start(bf16[8,256,128]{2,1,0:T(8,128)(2,1)} %collective-permute-done.20), channel_id=1, source_target_pairs={{1,0},{2,1},{3,2},{4,3},{5,4},{6,5},{7,6},{8,7},{9,8},{10,9},{11,1... | collective-permute-start | bytes 1572872 | tf_op jit(solution)/shard_map/ppermute | solution.py:17
  71.4 14.9 %collective-permute-start.25 = (bf16[8,256,128]{2,1,0:T(8,128)(2,1)}, bf16[8,256,128]{2,1,0:T(8,128)(2,1)S(1)}, u32[]{:S(2)}, u32[]{:S(2)}) collective-permute-start(bf16[8,256,128]{2,1,0:T(8,128)(2,1)} %collective-permute-done.22), channel_id=1, source_target_pairs={{1,0},{2,1},{3,2},{4,3},{5,4},{6,5},{7,6},{8,7},{9,8},{10,9},{11,1... | collective-permute-start | bytes 1572872 | tf_op jit(solution)/shard_map/ppermute | solution.py:17
  75.2 18.6 %collective-permute-start.4 = (bf16[8,256,128]{2,1,0:T(8,128)(2,1)S(1)}, bf16[8,256,128]{2,1,0:T(8,128)(2,1)S(1)}, u32[]{:S(2)}, u32[]{:S(2)}) collective-permute-start(bf16[8,256,128]{2,1,0:T(8,128)(2,1)S(1)} %collective-permute-done.3), channel_id=1, source_target_pairs={{0,1},{1,2},{2,3},{3,4},{4,5},{5,6},{6,7},{7,8},{8,9},{9,10},{10,1... | collective-permute-start | bytes 1572872 | tf_op jit(solution)/shard_map/ppermute | solution.py:17
  78.4 17.9 %collective-permute-start.26 = (bf16[8,256,128]{2,1,0:T(8,128)(2,1)S(1)}, bf16[8,256,128]{2,1,0:T(8,128)(2,1)S(1)}, u32[]{:S(2)}, u32[]{:S(2)}) collective-permute-start(bf16[8,256,128]{2,1,0:T(8,128)(2,1)S(1)} %collective-permute-done.23), channel_id=1, source_target_pairs={{1,0},{2,1},{3,2},{4,3},{5,4},{6,5},{7,6},{8,7},{9,8},{10,9},{11,1... | collective-permute-start | bytes 1572872 | tf_op jit(solution)/shard_map/ppermute | solution.py:17
  86.4 17.8 %collective-permute-start.28 = (bf16[8,256,128]{2,1,0:T(8,128)(2,1)S(1)}, bf16[8,256,128]{2,1,0:T(8,128)(2,1)S(1)}, u32[]{:S(2)}, u32[]{:S(2)}) collective-permute-start(bf16[8,256,128]{2,1,0:T(8,128)(2,1)S(1)} %collective-permute-done.25), channel_id=1, source_target_pairs={{1,0},{2,1},{3,2},{4,3},{5,4},{6,5},{7,6},{8,7},{9,8},{10,9},{11,1... | collective-permute-start | bytes 1572872 | tf_op jit(solution)/shard_map/ppermute | solution.py:17
  93.8 14.7 %collective-permute-start.5 = (bf16[8,256,128]{2,1,0:T(8,128)(2,1)S(1)}, bf16[8,256,128]{2,1,0:T(8,128)(2,1)S(1)}, u32[]{:S(2)}, u32[]{:S(2)}) collective-permute-start(bf16[8,256,128]{2,1,0:T(8,128)(2,1)S(1)} %collective-permute-done.4), channel_id=1, source_target_pairs={{0,1},{1,2},{2,3},{3,4},{4,5},{5,6},{6,7},{7,8},{8,9},{9,10},{10,1... | collective-permute-start | bytes 1572872 | tf_op jit(solution)/shard_map/ppermute | solution.py:17
  108.6 16.9 %collective-permute-start.6 = (bf16[8,256,128]{2,1,0:T(8,128)(2,1)S(1)}, bf16[8,256,128]{2,1,0:T(8,128)(2,1)S(1)}, u32[]{:S(2)}, u32[]{:S(2)}) collective-permute-start(bf16[8,256,128]{2,1,0:T(8,128)(2,1)S(1)} %collective-permute-done.5), channel_id=1, source_target_pairs={{0,1},{1,2},{2,3},{3,4},{4,5},{5,6},{6,7},{7,8},{8,9},{9,10},{10,1... | collective-permute-start | bytes 1572872 | tf_op jit(solution)/shard_map/ppermute | solution.py:17
  110.8 59.8 %collective-permute-start.32 = (bf16[8,256,128]{2,1,0:T(8,128)(2,1)S(1)}, bf16[8,256,128]{2,1,0:T(8,128)(2,1)S(1)}, u32[]{:S(2)}, u32[]{:S(2)}) collective-permute-start(bf16[8,256,128]{2,1,0:T(8,128)(2,1)S(1)} %collective-permute-done.29), channel_id=1, source_target_pairs={{1,0},{2,1},{3,2},{4,3},{5,4},{6,5},{7,6},{8,7},{9,8},{10,9},{11,1... | collective-permute-start | bytes 1572872 | tf_op jit(solution)/shard_map/ppermute | solution.py:17
  118.9 53.8 %collective-permute-start.34 = (bf16[8,256,128]{2,1,0:T(8,128)(2,1)S(1)}, bf16[8,256,128]{2,1,0:T(8,128)(2,1)S(1)}, u32[]{:S(2)}, u32[]{:S(2)}) collective-permute-start(bf16[8,256,128]{2,1,0:T(8,128)(2,1)S(1)} %collective-permute-done.31), channel_id=1, source_target_pairs={{1,0},{2,1},{3,2},{4,3},{5,4},{6,5},{7,6},{8,7},{9,8},{10,9},{11,1... | collective-permute-start | bytes 1572872 | tf_op jit(solution)/shard_map/ppermute | solution.py:17
  144.7 25.9 %collective-permute-start.33 = (f32[8,512]{1,0:T(8,128)S(1)}, f32[8,512]{1,0:T(8,128)S(1)}, u32[]{:S(2)}, u32[]{:S(2)}) collective-permute-start(f32[8,512]{1,0:T(8,128)S(1)} %pad_maximum_fusion), channel_id=1, source_target_pairs={{7,0},{8,1},{9,2},{10,3},{11,4},{12,5},{13,6},{14,7},{15,8},{16,9}... | collective-permute-start | bytes 49160 | tf_op jit(solution)/shard_map/ppermute | solution.py:17
  146.6 46.0 %collective-permute-start.7 = (bf16[8,256,128]{2,1,0:T(8,128)(2,1)S(1)}, bf16[8,256,128]{2,1,0:T(8,128)(2,1)}, u32[]{:S(2)}, u32[]{:S(2)}) collective-permute-start(bf16[8,256,128]{2,1,0:T(8,128)(2,1)S(1)} %bitcast.262), channel_id=1, source_target_pairs={{0,1},{1,2},{2,3},{3,4},{4,5},{5,6},{6,7},{7,8},{8,9},{9,10},{10,1... | collective-permute-start | bytes 1572872 | tf_op jit(solution)/shard_map/ppermute | solution.py:17
  192.6 15.0 %collective-permute-start.8 = (bf16[8,256,128]{2,1,0:T(8,128)(2,1)}, bf16[8,256,128]{2,1,0:T(8,128)(2,1)S(1)}, u32[]{:S(2)}, u32[]{:S(2)}) collective-permute-start(bf16[8,256,128]{2,1,0:T(8,128)(2,1)} %collective-permute-done.7), channel_id=1, source_target_pairs={{0,1},{1,2},{2,3},{3,4},{4,5},{5,6},{6,7},{7,8},{8,9},{9,10},{10,1... | collective-permute-start | bytes 1572872 | tf_op jit(solution)/shard_map/ppermute | solution.py:17
  207.7 14.7 %collective-permute-start.9 = (bf16[8,256,128]{2,1,0:T(8,128)(2,1)S(1)}, bf16[8,256,128]{2,1,0:T(8,128)(2,1)S(1)}, u32[]{:S(2)}, u32[]{:S(2)}) collective-permute-start(bf16[8,256,128]{2,1,0:T(8,128)(2,1)S(1)} %collective-permute-done.8), channel_id=1, source_target_pairs={{0,1},{1,2},{2,3},{3,4},{4,5},{5,6},{6,7},{7,8},{8,9},{9,10},{10,1... | collective-permute-start | bytes 1572872 | tf_op jit(solution)/shard_map/ppermute | solution.py:17
  251.8 14.7 %collective-permute-start.12 = (bf16[8,256,128]{2,1,0:T(8,128)(2,1)S(1)}, bf16[8,256,128]{2,1,0:T(8,128)(2,1)S(1)}, u32[]{:S(2)}, u32[]{:S(2)}) collective-permute-start(bf16[8,256,128]{2,1,0:T(8,128)(2,1)S(1)} %collective-permute-done.11), channel_id=1, source_target_pairs={{0,1},{1,2},{2,3},{3,4},{4,5},{5,6},{6,7},{7,8},{8,9},{9,10},{10,1... | collective-permute-start | bytes 1572872 | tf_op jit(solution)/shard_map/ppermute | solution.py:17
  (74 other events, 812.0 us)

commit v2 on v0

--- a/solution.py
+++ b/solution.py
@@ -61,13 +61,13 @@
 
     key_values = [(key_h, value_h)]
     query_grads = [(query_h, grad_h)]
-    moving_kv = (key_h, value_h)
-    moving_qg = (query_h, grad_h)
+    moving_kv = jnp.stack([key_h, value_h])
+    moving_qg = jnp.stack([query_h, grad_h])
     for step in range(1, window):
         moving_kv = from_behind(moving_kv, axes, 1)
         moving_qg = from_behind(moving_qg, axes, -1)
-        key_values.append(moving_kv)
-        query_grads.append(moving_qg)
+        key_values.append((moving_kv[0], moving_kv[1]))
+        query_grads.append((moving_qg[0], moving_qg[1]))
 
     def scores_of(q, k, mask):
         s = jnp.einsum("hqd,hkd->hqk", q, k, preferred_element_type=jnp.float32) * scale

time: 226 us -> 242 us (1.071)
  the two profiles are of different devices: /device:TPU:14 before, /device:TPU:15 now
where the time goes in v2:
time: 242 us; the launch traced here: 240 us
  starting transfers between devices  122 us (50%)
  matrix products  71.3 us (29%)
  waiting for transfers between devices  24.2 us (10%)
  local copies, waits for them, and re-layouts  12 us (5%)
  other arithmetic  8.29 us (3%)
    ppermute x21, starting transfers between devices, from_behind(): lax.ppermute(value, axis, [(source, source + steps) for source in range(f...  122 us
    ppermute x21, waiting for transfers between devices, from_behind(): lax.ppermute(value, axis, [(source, source + steps) for source in range(f...  24.2 us
    dot_general x7, matrix products, key_tile(): jnp.einsum('hkd,hqd->hkq', key_h, q_in, preferred_element_type=jnp.float32)  17.5 us
    unnamed x72, local copies, waits for them, and re-layouts  9.6 us
    dot_general x8, matrix products, tile_grads(): dprob = jnp.einsum('hqd,hkd->hqk', g, v, preferred_element_type=jnp.float32)  9.49 us
    dot_general x8, matrix products, scores_of(): jnp.einsum('hqd,hkd->hqk', q, k, preferred_element_type=jnp.float32) * scale  9.13 us
    dot_general x7, matrix products, key_tile(): jnp.einsum('hkd,hqd->hkq', value_h, g_in, preferred_element_type=jnp.floa...  9 us
    dot_general x7, matrix products, key_tile(): jnp.einsum('hkq,hqd->hkd', prob_b, g_in, preferred_element_type=jnp.float32)  8.46 us
  transfers between devices with their start and end apart: 21, of which 8 were waited for; matrix products, arithmetic and copies ran while one was open for 26% of the time, Pallas kernels for 0%

profile of v2, /device:TPU:15, one launch (start us, length us, event | category | flops | bytes accessed | tf_op | source)
XLA Modules:
  0.0 239.9 jit_solution(10393255082267568467)
XLA Ops:
  3.8 4.1 %collective-permute-start = (bf16[2,8,256,128]{3,2,1,0:T(8,128)(2,1)}, bf16[2,8,256,128]{3,2,1,0:T(8,128)(2,1)}, u32[]{:S(2)}, u32[]{:S(2)}) collective-permute-start(bf16[2,8,256,128]{3,2,1,0:T(8,128)(2,1)} %pad_maximum_fusion), channel_id=1, source_target_pairs={{0,1},{1,2},{2,3},{3,4},{4,5},{5,6},{6,7},{7,8},{8,9},{9,10},{10,1... | collective-permute-start | bytes 3145736 | tf_op jit(solution)/shard_map/ppermute | solution.py:17
  13.0 7.0 %collective-permute-done = bf16[2,8,256,128]{3,2,1,0:T(8,128)(2,1)} collective-permute-done((bf16[2,8,256,128]{3,2,1,0:T(8,128)(2,1)}, bf16[2,8,256,128]{3,2,1,0:T(8,128)(2,1)}, u32[]{:S(2)}, u32[]{:S(2)}) %collective-permute-start) | collective-permute-done | bytes 1048608 | tf_op jit(solution)/shard_map/ppermute | solution.py:17
  20.0 4.4 %collective-permute-start.1 = (bf16[2,8,256,128]{3,2,1,0:T(8,128)(2,1)}, bf16[2,8,256,128]{3,2,1,0:T(8,128)(2,1)}, u32[]{:S(2)}, u32[]{:S(2)}) collective-permute-start(bf16[2,8,256,128]{3,2,1,0:T(8,128)(2,1)} %collective-permute-done), channel_id=1, source_target_pairs={{0,1},{1,2},{2,3},{3,4},{4,5},{5,6},{6,7},{7,8},{8,9},{9,10},{10,1... | collective-permute-start | bytes 3145736 | tf_op jit(solution)/shard_map/ppermute | solution.py:17
  27.5 3.7 %collective-permute-start.9 = (bf16[2,8,256,128]{3,2,1,0:T(8,128)(2,1)}, bf16[2,8,256,128]{3,2,1,0:T(8,128)(2,1)S(1)}, u32[]{:S(2)}, u32[]{:S(2)}) collective-permute-start(bf16[2,8,256,128]{3,2,1,0:T(8,128)(2,1)} %collective-permute-done.7), channel_id=1, source_target_pairs={{1,0},{2,1},{3,2},{4,3},{5,4},{6,5},{7,6},{8,7},{9,8},{10,9},{11,1... | collective-permute-start | bytes 3145736 | tf_op jit(solution)/shard_map/ppermute | solution.py:17
  31.9 4.5 %collective-permute-done.1 = bf16[2,8,256,128]{3,2,1,0:T(8,128)(2,1)} collective-permute-done((bf16[2,8,256,128]{3,2,1,0:T(8,128)(2,1)}, bf16[2,8,256,128]{3,2,1,0:T(8,128)(2,1)}, u32[]{:S(2)}, u32[]{:S(2)}) %collective-permute-start.1) | collective-permute-done | bytes 1048608 | tf_op jit(solution)/shard_map/ppermute | solution.py:17
  36.4 4.4 %collective-permute-start.2 = (bf16[2,8,256,128]{3,2,1,0:T(8,128)(2,1)}, bf16[2,8,256,128]{3,2,1,0:T(8,128)(2,1)S(1)}, u32[]{:S(2)}, u32[]{:S(2)}) collective-permute-start(bf16[2,8,256,128]{3,2,1,0:T(8,128)(2,1)} %collective-permute-done.1), channel_id=1, source_target_pairs={{0,1},{1,2},{2,3},{3,4},{4,5},{5,6},{6,7},{7,8},{8,9},{9,10},{10,1... | collective-permute-start | bytes 3145736 | tf_op jit(solution)/shard_map/ppermute | solution.py:17
  41.0 2.8 %collective-permute-done.9 = bf16[2,8,256,128]{3,2,1,0:T(8,128)(2,1)S(1)} collective-permute-done((bf16[2,8,256,128]{3,2,1,0:T(8,128)(2,1)}, bf16[2,8,256,128]{3,2,1,0:T(8,128)(2,1)S(1)}, u32[]{:S(2)}, u32[]{:S(2)}) %collective-permute-start.9) | collective-permute-done | bytes 1048608 | tf_op jit(solution)/shard_map/ppermute | solution.py:17
  43.8 5.9 %collective-permute-start.11 = (bf16[2,8,256,128]{3,2,1,0:T(8,128)(2,1)S(1)}, bf16[2,8,256,128]{3,2,1,0:T(8,128)(2,1)}, u32[]{:S(2)}, u32[]{:S(2)}) collective-permute-start(bf16[2,8,256,128]{3,2,1,0:T(8,128)(2,1)S(1)} %collective-permute-done.9), channel_id=1, source_target_pairs={{1,0},{2,1},{3,2},{4,3},{5,4},{6,5},{7,6},{8,7},{9,8},{10,9},{11,1... | collective-permute-start | bytes 3145736 | tf_op jit(solution)/shard_map/ppermute | solution.py:17
  49.8 3.0 %collective-permute-done.2 = bf16[2,8,256,128]{3,2,1,0:T(8,128)(2,1)S(1)} collective-permute-done((bf16[2,8,256,128]{3,2,1,0:T(8,128)(2,1)}, bf16[2,8,256,128]{3,2,1,0:T(8,128)(2,1)S(1)}, u32[]{:S(2)}, u32[]{:S(2)}) %collective-permute-start.2) | collective-permute-done | bytes 1048608 | tf_op jit(solution)/shard_map/ppermute | solution.py:17
  52.8 4.3 %collective-permute-start.3 = (bf16[2,8,256,128]{3,2,1,0:T(8,128)(2,1)S(1)}, bf16[2,8,256,128]{3,2,1,0:T(8,128)(2,1)}, u32[]{:S(2)}, u32[]{:S(2)}) collective-permute-start(bf16[2,8,256,128]{3,2,1,0:T(8,128)(2,1)S(1)} %collective-permute-done.2), channel_id=1, source_target_pairs={{0,1},{1,2},{2,3},{3,4},{4,5},{5,6},{6,7},{7,8},{8,9},{9,10},{10,1... | collective-permute-start | bytes 3145736 | tf_op jit(solution)/shard_map/ppermute | solution.py:17
  57.3 2.9 %collective-permute-done.11 = bf16[2,8,256,128]{3,2,1,0:T(8,128)(2,1)} collective-permute-done((bf16[2,8,256,128]{3,2,1,0:T(8,128)(2,1)S(1)}, bf16[2,8,256,128]{3,2,1,0:T(8,128)(2,1)}, u32[]{:S(2)}, u32[]{:S(2)}) %collective-permute-start.11) | collective-permute-done | bytes 1048608 | tf_op jit(solution)/shard_map/ppermute | solution.py:17
  60.2 7.6 %collective-permute-start.13 = (bf16[2,8,256,128]{3,2,1,0:T(8,128)(2,1)}, bf16[2,8,256,128]{3,2,1,0:T(8,128)(2,1)}, u32[]{:S(2)}, u32[]{:S(2)}) collective-permute-start(bf16[2,8,256,128]{3,2,1,0:T(8,128)(2,1)} %collective-permute-done.11), channel_id=1, source_target_pairs={{1,0},{2,1},{3,2},{4,3},{5,4},{6,5},{7,6},{8,7},{9,8},{10,9},{11,1... | collective-permute-start | bytes 3145736 | tf_op jit(solution)/shard_map/ppermute | solution.py:17
  70.5 2.8 %collective-permute-start.4 = (bf16[2,8,256,128]{3,2,1,0:T(8,128)(2,1)}, bf16[2,8,256,128]{3,2,1,0:T(8,128)(2,1)}, u32[]{:S(2)}, u32[]{:S(2)}) collective-permute-start(bf16[2,8,256,128]{3,2,1,0:T(8,128)(2,1)} %collective-permute-done.3), channel_id=1, source_target_pairs={{0,1},{1,2},{2,3},{3,4},{4,5},{5,6},{6,7},{7,8},{8,9},{9,10},{10,1... | collective-permute-start | bytes 3145736 | tf_op jit(solution)/shard_map/ppermute | solution.py:17
  76.9 9.5 %collective-permute-start.15 = (bf16[2,8,256,128]{3,2,1,0:T(8,128)(2,1)}, bf16[2,8,256,128]{3,2,1,0:T(8,128)(2,1)S(1)}, u32[]{:S(2)}, u32[]{:S(2)}) collective-permute-start(bf16[2,8,256,128]{3,2,1,0:T(8,128)(2,1)} %collective-permute-done.13), channel_id=1, source_target_pairs={{1,0},{2,1},{3,2},{4,3},{5,4},{6,5},{7,6},{8,7},{9,8},{10,9},{11,1... | collective-permute-start | bytes 3145736 | tf_op jit(solution)/shard_map/ppermute | solution.py:17
  93.6 11.3 %collective-permute-start.17 = (bf16[2,8,256,128]{3,2,1,0:T(8,128)(2,1)S(1)}, bf16[2,8,256,128]{3,2,1,0:T(8,128)(2,1)}, u32[]{:S(2)}, u32[]{:S(2)}) collective-permute-start(bf16[2,8,256,128]{3,2,1,0:T(8,128)(2,1)S(1)} %collective-permute-done.15), channel_id=1, source_target_pairs={{1,0},{2,1},{3,2},{4,3},{5,4},{6,5},{7,6},{8,7},{9,8},{10,9},{11,1... | collective-permute-start | bytes 3145736 | tf_op jit(solution)/shard_map/ppermute | solution.py:17
  110.9 12.4 %collective-permute-start.19 = (bf16[2,8,256,128]{3,2,1,0:T(8,128)(2,1)}, bf16[2,8,256,128]{3,2,1,0:T(8,128)(2,1)}, u32[]{:S(2)}, u32[]{:S(2)}) collective-permute-start(bf16[2,8,256,128]{3,2,1,0:T(8,128)(2,1)} %collective-permute-done.17), channel_id=1, source_target_pairs={{1,0},{2,1},{3,2},{4,3},{5,4},{6,5},{7,6},{8,7},{9,8},{10,9},{11,1... | collective-permute-start | bytes 3145736 | tf_op jit(solution)/shard_map/ppermute | solution.py:17
  126.0 12.7 %collective-permute-start.8 = (f32[8,512]{1,0:T(8,128)S(1)}, f32[8,512]{1,0:T(8,128)S(1)}, u32[]{:S(2)}, u32[]{:S(2)}) collective-permute-start(f32[8,512]{1,0:T(8,128)S(1)} %pad_maximum_fusion.2), channel_id=1, source_target_pairs={{1,0},{2,1},{3,2},{4,3},{5,4},{6,5},{7,6},{8,7},{9,8},{10,9},{11,1... | collective-permute-start | bytes 49160 | tf_op jit(solution)/shard_map/ppermute | solution.py:17
  164.4 6.6 %collective-permute-start.16 = (f32[8,512]{1,0:T(8,128)S(1)}, f32[8,512]{1,0:T(8,128)S(1)}, u32[]{:S(2)}, u32[]{:S(2)}) collective-permute-start(f32[8,512]{1,0:T(8,128)S(1)} %pad_maximum_fusion.2), channel_id=1, source_target_pairs={{5,0},{6,1},{7,2},{8,3},{9,4},{10,5},{11,6},{12,7},{13,8},{14,9},{... | collective-permute-start | bytes 49160 | tf_op jit(solution)/shard_map/ppermute | solution.py:17
  171.0 19.0 %collective-permute-start.18 = (f32[8,512]{1,0:T(8,128)S(1)}, f32[8,512]{1,0:T(8,128)S(1)}, u32[]{:S(2)}, u32[]{:S(2)}) collective-permute-start(f32[8,512]{1,0:T(8,128)S(1)} %pad_maximum_fusion.2), channel_id=1, source_target_pairs={{6,0},{7,1},{8,2},{9,3},{10,4},{11,5},{12,6},{13,7},{14,8},{15,9},... | collective-permute-start | bytes 49160 | tf_op jit(solution)/shard_map/ppermute | solution.py:17
  192.4 2.9 %fusion.36 = (bf16[8,256,256]{1,2,0:T(8,128)(2,1)}, f32[8,256,256]{2,1,0:T(8,128)S(1)}) fusion(f32[8,256]{1,0:T(8,128)S(1)} %get-tuple-element.57, pred[256,256]{0,1:T(8,128)(4,1)S(1)} %copy-done.25, bf16[256,8,128]{2,0,1:T(8,128)(2,1)S(1)} %copy-done.1, bf16[2,8,256,128]{3,2,1,0:T(8,128)(2,1)} %collective-permute-done.7), kind=kOutput, calls=%fused_computation.75 | convolution fusion | flops 136839168 | bytes 4268032 | tf_op jit(solution)/shard_map/hkd,hqd->hkq/dot_general | solution.py:121
  197.9 2.8 %fusion.107 = (bf16[8,256,256]{1,2,0:T(8,128)(2,1)}, f32[8,256,256]{1,2,0:T(8,128)S(1)}) fusion(f32[8,256]{1,0:T(8,128)S(1)} %get-tuple-element.53, bf16[256,8,128]{2,0,1:T(8,128)(2,1)S(1)} %copy-done.1, bf16[2,8,256,128]{3,2,1,0:T(8,128)(2,1)} %collective-permute-done.11, pred[256,256]{0,1:T(8,128)(4,1)S(1)} %copy-done.29), kind=kOutput, calls=%fused_computation.241 | convolution fusion | flops 136839168 | bytes 4268032 | tf_op jit(solution)/shard_map/hkd,hqd->hkq/dot_general | solution.py:121
  202.2 2.8 %fusion.108 = (bf16[8,256,256]{1,2,0:T(8,128)(2,1)}, f32[8,256,256]{1,2,0:T(8,128)S(1)}) fusion(f32[8,256]{1,0:T(8,128)S(1)} %get-tuple-element.51, bf16[256,8,128]{2,0,1:T(8,128)(2,1)S(1)} %copy-done.1, bf16[2,8,256,128]{3,2,1,0:T(8,128)(2,1)} %collective-permute-done.13, pred[256,256]{0,1:T(8,128)(4,1)S(1)} %copy-done.28), kind=kOutput, calls=%fused_computation.242 | convolution fusion | flops 136839168 | bytes 4268032 | tf_op jit(solution)/shard_map/hkd,hqd->hkq/dot_general | solution.py:121
  208.3 2.7 %fusion.110 = (bf16[8,256,256]{1,2,0:T(8,128)(2,1)}, f32[8,256,256]{1,2,0:T(8,128)S(1)}) fusion(f32[8,256]{1,0:T(8,128)S(1)} %get-tuple-element.47, bf16[256,8,128]{2,0,1:T(8,128)(2,1)S(1)} %copy-done.1, bf16[2,8,256,128]{3,2,1,0:T(8,128)(2,1)} %collective-permute-done.17, pred[256,256]{0,1:T(8,128)(4,1)S(1)} %copy-done.26), kind=kOutput, calls=%fused_computation.244 | convolution fusion | flops 136839168 | bytes 4268032 | tf_op jit(solution)/shard_map/hkd,hqd->hkq/dot_general | solution.py:121
  215.0 2.8 %fusion.111 = (bf16[8,256,256]{1,2,0:T(8,128)(2,1)}, f32[8,256,256]{1,2,0:T(8,128)S(1)}) fusion(f32[8,256]{1,0:T(8,128)S(1)} %get-tuple-element.45, bf16[256,8,128]{2,0,1:T(8,128)(2,1)S(1)} %copy-done.1, bf16[2,8,256,128]{3,2,1,0:T(8,128)(2,1)} %collective-permute-done.19, pred[256,256]{0,1:T(8,128)(4,1)S(1)} %copy-done.24), kind=kOutput, calls=%fused_computation.245 | convolution fusion | flops 136839168 | bytes 4268032 | tf_op jit(solution)/shard_map/hkd,hqd->hkq/dot_general | solution.py:121
  (189 shorter events, 95.5 us)
Async XLA Ops:
  3.8 16.1 %collective-permute-start = (bf16[2,8,256,128]{3,2,1,0:T(8,128)(2,1)}, bf16[2,8,256,128]{3,2,1,0:T(8,128)(2,1)}, u32[]{:S(2)}, u32[]{:S(2)}) collective-permute-start(bf16[2,8,256,128]{3,2,1,0:T(8,128)(2,1)} %pad_maximum_fusion), channel_id=1, source_target_pairs={{0,1},{1,2},{2,3},{3,4},{4,5},{5,6},{6,7},{7,8},{8,9},{9,10},{10,1... | collective-permute-start | bytes 3145736 | tf_op jit(solution)/shard_map/ppermute | solution.py:17
  11.0 16.4 %collective-permute-start.7 = (bf16[2,8,256,128]{3,2,1,0:T(8,128)(2,1)}, bf16[2,8,256,128]{3,2,1,0:T(8,128)(2,1)}, u32[]{:S(2)}, u32[]{:S(2)}) collective-permute-start(bf16[2,8,256,128]{3,2,1,0:T(8,128)(2,1)} %pad_maximum_fusion.1), channel_id=1, source_target_pairs={{1,0},{2,1},{3,2},{4,3},{5,4},{6,5},{7,6},{8,7},{9,8},{10,9},{11,1... | collective-permute-start | bytes 3145736 | tf_op jit(solution)/shard_map/ppermute | solution.py:17
  20.0 16.4 %collective-permute-start.1 = (bf16[2,8,256,128]{3,2,1,0:T(8,128)(2,1)}, bf16[2,8,256,128]{3,2,1,0:T(8,128)(2,1)}, u32[]{:S(2)}, u32[]{:S(2)}) collective-permute-start(bf16[2,8,256,128]{3,2,1,0:T(8,128)(2,1)} %collective-permute-done), channel_id=1, source_target_pairs={{0,1},{1,2},{2,3},{3,4},{4,5},{5,6},{6,7},{7,8},{8,9},{9,10},{10,1... | collective-permute-start | bytes 3145736 | tf_op jit(solution)/shard_map/ppermute | solution.py:17
  27.5 16.3 %collective-permute-start.9 = (bf16[2,8,256,128]{3,2,1,0:T(8,128)(2,1)}, bf16[2,8,256,128]{3,2,1,0:T(8,128)(2,1)S(1)}, u32[]{:S(2)}, u32[]{:S(2)}) collective-permute-start(bf16[2,8,256,128]{3,2,1,0:T(8,128)(2,1)} %collective-permute-done.7), channel_id=1, source_target_pairs={{1,0},{2,1},{3,2},{4,3},{5,4},{6,5},{7,6},{8,7},{9,8},{10,9},{11,1... | collective-permute-start | bytes 3145736 | tf_op jit(solution)/shard_map/ppermute | solution.py:17
  36.4 16.4 %collective-permute-start.2 = (bf16[2,8,256,128]{3,2,1,0:T(8,128)(2,1)}, bf16[2,8,256,128]{3,2,1,0:T(8,128)(2,1)S(1)}, u32[]{:S(2)}, u32[]{:S(2)}) collective-permute-start(bf16[2,8,256,128]{3,2,1,0:T(8,128)(2,1)} %collective-permute-done.1), channel_id=1, source_target_pairs={{0,1},{1,2},{2,3},{3,4},{4,5},{5,6},{6,7},{7,8},{8,9},{9,10},{10,1... | collective-permute-start | bytes 3145736 | tf_op jit(solution)/shard_map/ppermute | solution.py:17
  43.8 16.4 %collective-permute-start.11 = (bf16[2,8,256,128]{3,2,1,0:T(8,128)(2,1)S(1)}, bf16[2,8,256,128]{3,2,1,0:T(8,128)(2,1)}, u32[]{:S(2)}, u32[]{:S(2)}) collective-permute-start(bf16[2,8,256,128]{3,2,1,0:T(8,128)(2,1)S(1)} %collective-permute-done.9), channel_id=1, source_target_pairs={{1,0},{2,1},{3,2},{4,3},{5,4},{6,5},{7,6},{8,7},{9,8},{10,9},{11,1... | collective-permute-start | bytes 3145736 | tf_op jit(solution)/shard_map/ppermute | solution.py:17
  52.8 16.2 %copy-start.10 = (bf16[2,8,256,128]{3,2,1,0:T(8,128)(2,1)}, bf16[2,8,256,128]{3,2,1,0:T(8,128)(2,1)S(1)}, u32[]{:S(2)}) copy-start(bf16[2,8,256,128]{3,2,1,0:T(8,128)(2,1)S(1)} %collective-permute-done.2) | copy-start | bytes 3145732
  52.8 17.7 %collective-permute-start.3 = (bf16[2,8,256,128]{3,2,1,0:T(8,128)(2,1)S(1)}, bf16[2,8,256,128]{3,2,1,0:T(8,128)(2,1)}, u32[]{:S(2)}, u32[]{:S(2)}) collective-permute-start(bf16[2,8,256,128]{3,2,1,0:T(8,128)(2,1)S(1)} %collective-permute-done.2), channel_id=1, source_target_pairs={{0,1},{1,2},{2,3},{3,4},{4,5},{5,6},{6,7},{7,8},{8,9},{9,10},{10,1... | collective-permute-start | bytes 3145736 | tf_op jit(solution)/shard_map/ppermute | solution.py:17
  60.2 16.7 %collective-permute-start.13 = (bf16[2,8,256,128]{3,2,1,0:T(8,128)(2,1)}, bf16[2,8,256,128]{3,2,1,0:T(8,128)(2,1)}, u32[]{:S(2)}, u32[]{:S(2)}) collective-permute-start(bf16[2,8,256,128]{3,2,1,0:T(8,128)(2,1)} %collective-permute-done.11), channel_id=1, source_target_pairs={{1,0},{2,1},{3,2},{4,3},{5,4},{6,5},{7,6},{8,7},{9,8},{10,9},{11,1... | collective-permute-start | bytes 3145736 | tf_op jit(solution)/shard_map/ppermute | solution.py:17
  70.5 17.8 %collective-permute-start.4 = (bf16[2,8,256,128]{3,2,1,0:T(8,128)(2,1)}, bf16[2,8,256,128]{3,2,1,0:T(8,128)(2,1)}, u32[]{:S(2)}, u32[]{:S(2)}) collective-permute-start(bf16[2,8,256,128]{3,2,1,0:T(8,128)(2,1)} %collective-permute-done.3), channel_id=1, source_target_pairs={{0,1},{1,2},{2,3},{3,4},{4,5},{5,6},{6,7},{7,8},{8,9},{9,10},{10,1... | collective-permute-start | bytes 3145736 | tf_op jit(solution)/shard_map/ppermute | solution.py:17
  76.9 16.7 %collective-permute-start.15 = (bf16[2,8,256,128]{3,2,1,0:T(8,128)(2,1)}, bf16[2,8,256,128]{3,2,1,0:T(8,128)(2,1)S(1)}, u32[]{:S(2)}, u32[]{:S(2)}) collective-permute-start(bf16[2,8,256,128]{3,2,1,0:T(8,128)(2,1)} %collective-permute-done.13), channel_id=1, source_target_pairs={{1,0},{2,1},{3,2},{4,3},{5,4},{6,5},{7,6},{8,7},{9,8},{10,9},{11,1... | collective-permute-start | bytes 3145736 | tf_op jit(solution)/shard_map/ppermute | solution.py:17
  88.3 18.5 %collective-permute-start.5 = (bf16[2,8,256,128]{3,2,1,0:T(8,128)(2,1)}, bf16[2,8,256,128]{3,2,1,0:T(8,128)(2,1)S(1)}, u32[]{:S(2)}, u32[]{:S(2)}) collective-permute-start(bf16[2,8,256,128]{3,2,1,0:T(8,128)(2,1)} %collective-permute-done.4), channel_id=1, source_target_pairs={{0,1},{1,2},{2,3},{3,4},{4,5},{5,6},{6,7},{7,8},{8,9},{9,10},{10,1... | collective-permute-start | bytes 3145736 | tf_op jit(solution)/shard_map/ppermute | solution.py:17
  93.6 17.2 %collective-permute-start.17 = (bf16[2,8,256,128]{3,2,1,0:T(8,128)(2,1)S(1)}, bf16[2,8,256,128]{3,2,1,0:T(8,128)(2,1)}, u32[]{:S(2)}, u32[]{:S(2)}) collective-permute-start(bf16[2,8,256,128]{3,2,1,0:T(8,128)(2,1)S(1)} %collective-permute-done.15), channel_id=1, source_target_pairs={{1,0},{2,1},{3,2},{4,3},{5,4},{6,5},{7,6},{8,7},{9,8},{10,9},{11,1... | collective-permute-start | bytes 3145736 | tf_op jit(solution)/shard_map/ppermute | solution.py:17
  106.8 17.2 %collective-permute-start.6 = (bf16[2,8,256,128]{3,2,1,0:T(8,128)(2,1)S(1)}, bf16[2,8,256,128]{3,2,1,0:T(8,128)(2,1)S(1)}, u32[]{:S(2)}, u32[]{:S(2)}) collective-permute-start(bf16[2,8,256,128]{3,2,1,0:T(8,128)(2,1)S(1)} %collective-permute-done.5), channel_id=1, source_target_pairs={{0,1},{1,2},{2,3},{3,4},{4,5},{5,6},{6,7},{7,8},{8,9},{9,10},{10,1... | collective-permute-start | bytes 3145736 | tf_op jit(solution)/shard_map/ppermute | solution.py:17
  110.9 104.1 %collective-permute-start.19 = (bf16[2,8,256,128]{3,2,1,0:T(8,128)(2,1)}, bf16[2,8,256,128]{3,2,1,0:T(8,128)(2,1)}, u32[]{:S(2)}, u32[]{:S(2)}) collective-permute-start(bf16[2,8,256,128]{3,2,1,0:T(8,128)(2,1)} %collective-permute-done.17), channel_id=1, source_target_pairs={{1,0},{2,1},{3,2},{4,3},{5,4},{6,5},{7,6},{8,7},{9,8},{10,9},{11,1... | collective-permute-start | bytes 3145736 | tf_op jit(solution)/shard_map/ppermute | solution.py:17
  126.0 38.4 %collective-permute-start.8 = (f32[8,512]{1,0:T(8,128)S(1)}, f32[8,512]{1,0:T(8,128)S(1)}, u32[]{:S(2)}, u32[]{:S(2)}) collective-permute-start(f32[8,512]{1,0:T(8,128)S(1)} %pad_maximum_fusion.2), channel_id=1, source_target_pairs={{1,0},{2,1},{3,2},{4,3},{5,4},{6,5},{7,6},{8,7},{9,8},{10,9},{11,1... | collective-permute-start | bytes 49160 | tf_op jit(solution)/shard_map/ppermute | solution.py:17
  138.7 32.3 %collective-permute-start.10 = (f32[8,512]{1,0:T(8,128)S(1)}, f32[8,512]{1,0:T(8,128)S(1)}, u32[]{:S(2)}, u32[]{:S(2)}) collective-permute-start(f32[8,512]{1,0:T(8,128)S(1)} %pad_maximum_fusion.2), channel_id=1, source_target_pairs={{2,0},{3,1},{4,2},{5,3},{6,4},{7,5},{8,6},{9,7},{10,8},{11,9},{12,... | collective-permute-start | bytes 49160 | tf_op jit(solution)/shard_map/ppermute | solution.py:17
  140.6 49.4 %collective-permute-start.12 = (f32[8,512]{1,0:T(8,128)S(1)}, f32[8,512]{1,0:T(8,128)S(1)}, u32[]{:S(2)}, u32[]{:S(2)}) collective-permute-start(f32[8,512]{1,0:T(8,128)S(1)} %pad_maximum_fusion.2), channel_id=1, source_target_pairs={{3,0},{4,1},{5,2},{6,3},{7,4},{8,5},{9,6},{10,7},{11,8},{12,9},{13... | collective-permute-start | bytes 49160 | tf_op jit(solution)/shard_map/ppermute | solution.py:17
  142.5 49.7 %collective-permute-start.14 = (f32[8,512]{1,0:T(8,128)S(1)}, f32[8,512]{1,0:T(8,128)S(1)}, u32[]{:S(2)}, u32[]{:S(2)}) collective-permute-start(f32[8,512]{1,0:T(8,128)S(1)} %pad_maximum_fusion.2), channel_id=1, source_target_pairs={{4,0},{5,1},{6,2},{7,3},{8,4},{9,5},{10,6},{11,7},{12,8},{13,9},{1... | collective-permute-start | bytes 49160 | tf_op jit(solution)/shard_map/ppermute | solution.py:17
  161.8 30.5 %copy-start.1 = (bf16[256,8,128]{2,0,1:T(8,128)(2,1)S(1)}, bf16[256,8,128]{2,0,1:T(8,128)(2,1)}, u32[]{:S(2)}) copy-start(bf16[256,8,128]{2,0,1:T(8,128)(2,1)} %copy-done) | copy-start | bytes 1572868
  161.8 30.5 %copy-start.25 = (pred[256,256]{0,1:T(8,128)(4,1)S(1)}, pred[256,256]{0,1:T(8,128)(4,1)}, u32[]{:S(2)}) copy-start(pred[256,256]{0,1:T(8,128)(4,1)} %get-tuple-element.65) | copy-start | bytes 196612
  164.4 27.9 %collective-permute-start.16 = (f32[8,512]{1,0:T(8,128)S(1)}, f32[8,512]{1,0:T(8,128)S(1)}, u32[]{:S(2)}, u32[]{:S(2)}) collective-permute-start(f32[8,512]{1,0:T(8,128)S(1)} %pad_maximum_fusion.2), channel_id=1, source_target_pairs={{5,0},{6,1},{7,2},{8,3},{9,4},{10,5},{11,6},{12,7},{13,8},{14,9},{... | collective-permute-start | bytes 49160 | tf_op jit(solution)/shard_map/ppermute | solution.py:17
  171.0 21.3 %collective-permute-start.18 = (f32[8,512]{1,0:T(8,128)S(1)}, f32[8,512]{1,0:T(8,128)S(1)}, u32[]{:S(2)}, u32[]{:S(2)}) collective-permute-start(f32[8,512]{1,0:T(8,128)S(1)} %pad_maximum_fusion.2), channel_id=1, source_target_pairs={{6,0},{7,1},{8,2},{9,3},{10,4},{11,5},{12,6},{13,7},{14,8},{15,9},... | collective-permute-start | bytes 49160 | tf_op jit(solution)/shard_map/ppermute | solution.py:17
  190.0 25.0 %collective-permute-start.20 = (f32[8,512]{1,0:T(8,128)S(1)}, f32[8,512]{1,0:T(8,128)S(1)}, u32[]{:S(2)}, u32[]{:S(2)}) collective-permute-start(f32[8,512]{1,0:T(8,128)S(1)} %pad_maximum_fusion.2), channel_id=1, source_target_pairs={{7,0},{8,1},{9,2},{10,3},{11,4},{12,5},{13,6},{14,7},{15,8},{16,9}... | collective-permute-start | bytes 49160 | tf_op jit(solution)/shard_map/ppermute | solution.py:17
  (29 other events, 115.9 us)
